TPU v7x, 256 devices: a whole 4x4x8 slice. The times are simulated.
256 devices in a mesh: gx: 8 (over z), gy: 4 (over x_lo, core), gz: 8 (over y, x_hi).
Axes of the slice: x: 4 (x_hi: 2, x_lo: 2; x = x_hi * 2 + x_lo), y: 4, z: 8, core: 2. Of those that a mesh axis runs over, the one named last changes fastest.
Arguments:
- displacement: float32 [3, 128, 32, 1024], P(None, 'gx', 'gy', 'gz'), may hold values from -3 to 3
- velocity: float32 [3, 128, 32, 1024], P(None, 'gx', 'gy', 'gz'), may hold values from -6 to 6
- bulk_modulus: float32 [128, 32, 1024], P('gx', 'gy', 'gz'), may hold values from 3000 to 20000
- shear_modulus: float32 [128, 32, 1024], P('gx', 'gy', 'gz'), may hold values from 300 to 1500
- blast_load: float32 [3, 128, 32, 1024], P(None, 'gx', 'gy', 'gz'), may hold values from -50 to 50
- loaded: int32 [128, 32, 1024], P('gx', 'gy', 'gz'), may hold values 0 or 1
- broken: int32 [16, 128, 32, 1024], P(None, 'gx', 'gy', 'gz'), may hold values from 0 to 255
Outputs:
- new_displacement: float32 [3, 128, 32, 1024], P(None, 'gx', 'gy', 'gz')
- new_velocity: float32 [3, 128, 32, 1024], P(None, 'gx', 'gy', 'gz')
Inputs may be any that keep to these rules, and one draw needn't show every extreme that they name: A bond's flag is the same at both of its ends: the flag of offset k at node i equals that of offset k + 61 at node i + o_k whenever that node lies in the lattice, for k under 61.
All inputs are finite; a program needn't handle non-finite values. No bound on the sum of `loaded` on one device may be relied on, other than what follows from the above.
Results may differ from a plain program's by a relative error of at most 0.0001.
Values sent between devices are 32-bit elements; how exact they have to be, the bound alone decides.
No kernel may reach another device: no remote copies, remote signals or barrier semaphores. Data moves between devices by JAX's collectives and lax.ppermute only.
A program may use at most 128 MiB of HBM per device.

v0:
```python
import math

import jax
import jax.numpy as jnp
from jax import lax
from jax.experimental import pallas as pl
from jax.experimental.pallas import tpu as pltpu
from jax.sharding import PartitionSpec as P

STEPS = 2


TIME_STEP = 0.01

INTERPRET = False

ROWS = 4


def extended_2(cells, sides, width):
    for axis, dim in sides:
        count = lax.axis_size(axis)
        ends = count - 1
        head = lax.slice_in_dim(cells, 0, width, axis=dim)
        tail = lax.slice_in_dim(cells, cells.shape[dim] - width, cells.shape[dim], axis=dim)
        cells = jnp.concatenate(
            [
                lax.ppermute(tail.reshape(-1), axis, [(i, (i + 1) % count) for i in range(ends)]).reshape(tail.shape),
                cells,
                lax.ppermute(head.reshape(-1), axis, [((i + 1) % count, i) for i in range(ends)]).reshape(head.shape),
            ],
            axis=dim,
        )
    return cells


def offset_table():
    forward = []
    for step_x in range(-3, 4):
        for step_y in range(-3, 4):
            for step_z in range(-3, 4):
                squared = step_x * step_x + step_y * step_y + step_z * step_z
                if squared == 0 or squared > 9:
                    continue
                summed = step_x + step_y + step_z
                if summed > 0 or (summed == 0 and (step_x > 0 or (step_x == 0 and step_y > 0))):
                    forward.append((step_x, step_y, step_z))
    backward = []
    for entry in forward:
        backward.append((-entry[0], -entry[1], -entry[2]))
    return forward + backward


OFFSETS = offset_table()
LENGTHS = [math.sqrt(e[0] ** 2 + e[1] ** 2 + e[2] ** 2) for e in OFFSETS]
PAIRS = sorted({(e[1], e[2]) for e in OFFSETS} | {(0, 0)})
PAIR_OF = {pair: number for number, pair in enumerate(PAIRS)}


def presence(cell_count, device_index, device_count, offset_value):
    position = device_index * cell_count + jnp.arange(cell_count, dtype=jnp.int32) + offset_value
    return ((position >= 0) & (position < device_count * cell_count)).astype(jnp.float32)


def extend(values):
    return extended_2(values, (("gx", 1), ("gy", 2), ("gz", 3)), 3)


def fill_stack(stack_ref, padded_ref, leading):
    cells_y, cells_z = stack_ref.shape[-2], stack_ref.shape[-1]

    def row(index, carry):
        for pair, (oy, oz) in enumerate(PAIRS):
            for c in leading:
                target = (pair, pl.ds(index, 1)) if c is None else (pair, c, pl.ds(index, 1))
                source = (pl.ds(index, 1),) if c is None else (c, pl.ds(index, 1))
                stack_ref[target] = padded_ref[source + (pl.ds(3 + oy, cells_y), pl.ds(3 + oz, cells_z))]
        return carry

    lax.fori_loop(0, stack_ref.shape[-3], row, 0)


def stretch_kernel(ext_ref, intact_ref, weight_ref, factor_ref, stretch_ref, coupling_ref, us_ref):
    block = pl.program_id(0)

    @pl.when(block == 0)
    def _():
        fill_stack(us_ref, ext_ref, (0, 1, 2))

    centre = PAIR_OF[(0, 0)]
    x0 = pl.multiple_of(block * ROWS, ROWS)
    own = [us_ref[centre, c, pl.ds(x0 + 3, ROWS)] for c in range(3)]
    total = jnp.zeros_like(own[0])
    for number, entry in enumerate(OFFSETS):
        pair = PAIR_OF[(entry[1], entry[2])]
        squared = None
        for c in range(3):
            diff = us_ref[pair, c, pl.ds(x0 + 3 + entry[0], ROWS)] - own[c]
            if entry[c] != 0:
                diff = diff + float(entry[c])
            squared = diff * diff if squared is None else squared + diff * diff
        value = jnp.sqrt(squared) - LENGTHS[number]
        stretch_ref[number] = value
        total = total + intact_ref[number] * LENGTHS[number] * value
    weight = weight_ref[...]
    dilatation = 3.0 * total / weight
    coupling_ref[...] = dilatation * factor_ref[...] / weight


def force_kernel(pc_ref, ps_ref, stretch_ref, intact_ref, u_ref, v_ref, load_ref, unew_ref, vnew_ref, cs_ref, ss_ref):
    block = pl.program_id(0)

    @pl.when(block == 0)
    def _():
        fill_stack(cs_ref, pc_ref, (None,))
        fill_stack(ss_ref, ps_ref, (None,))

    centre = PAIR_OF[(0, 0)]
    x0 = pl.multiple_of(block * ROWS, ROWS)
    c_own = cs_ref[centre, pl.ds(x0 + 3, ROWS)]
    s_own = ss_ref[centre, pl.ds(x0 + 3, ROWS)]
    force = [None, None, None]
    for number, entry in enumerate(OFFSETS):
        pair = PAIR_OF[(entry[1], entry[2])]
        rows = pl.ds(x0 + 3 + entry[0], ROWS)
        scalar = intact_ref[number] * (
            LENGTHS[number] * (c_own + cs_ref[pair, rows])
            + (s_own + ss_ref[pair, rows]) * stretch_ref[number]
        )
        for c in range(3):
            if entry[c] != 0:
                term = scalar * (entry[c] / LENGTHS[number])
                force[c] = term if force[c] is None else force[c] + term
    for c in range(3):
        v_new = v_ref[c] + TIME_STEP * (force[c] + load_ref[c])
        vnew_ref[c] = v_new
        unew_ref[c] = u_ref[c] + TIME_STEP * v_new


def compiler_params():
    return pltpu.CompilerParams(vmem_limit_bytes=100 * 1024 * 1024)


def local(displacement, velocity, bulk_modulus, shear_modulus, blast_load, loaded, broken):
    count = len(OFFSETS)
    cell_shape = displacement.shape[1:]
    cells_x, cells_y, cells_z = cell_shape
    index_x = lax.axis_index("gx")
    index_y = lax.axis_index("gy")
    index_z = lax.axis_index("gz")
    span_x = lax.axis_size("gx")
    span_y = lax.axis_size("gy")
    span_z = lax.axis_size("gz")
    along_x = {value: presence(cells_x, index_x, span_x, value) for value in range(-3, 4)}
    along_y = {value: presence(cells_y, index_y, span_y, value) for value in range(-3, 4)}
    along_z = {value: presence(cells_z, index_z, span_z, value) for value in range(-3, 4)}
    exists_x = jnp.stack([along_x[e[0]] for e in OFFSETS])
    exists_y = jnp.stack([along_y[e[1]] for e in OFFSETS])
    exists_z = jnp.stack([along_z[e[2]] for e in OFFSETS])
    exists = exists_x[:, :, None, None] * exists_y[:, None, :, None] * exists_z[:, None, None, :]
    squares = jnp.array([l * l for l in LENGTHS], jnp.float32)
    weight = jnp.sum(exists * squares[:, None, None, None], axis=0)
    shifts = jnp.arange(8, dtype=jnp.int32)
    bits = jnp.right_shift(broken[:, None], shifts[None, :, None, None, None]) & 1
    bits = bits.reshape((broken.shape[0] * 8,) + tuple(cell_shape))[:count]
    intact = exists * (1.0 - bits.astype(jnp.float32))
    stiffness = 15.0 * shear_modulus / weight
    load_force = loaded.astype(jnp.float32)[None] * blast_load
    modulus_factor = 3.0 * bulk_modulus - 5.0 * shear_modulus
    displacement_now = displacement
    velocity_now = velocity
    padded_stiffness = None
    f32 = jnp.float32
    pairs = len(PAIRS)
    halo_x = cells_x + 6

    def whole(shape):
        return pl.BlockSpec(shape, lambda block: (0,) * len(shape))

    bonds_spec = pl.BlockSpec((count, ROWS, cells_y, cells_z), lambda block: (0, block, 0, 0))
    cells_spec = pl.BlockSpec((ROWS, cells_y, cells_z), lambda block: (block, 0, 0))
    vector_spec = pl.BlockSpec((3, ROWS, cells_y, cells_z), lambda block: (0, block, 0, 0))
    for step_index in range(STEPS):
        if step_index == 0:
            extended = extend(jnp.concatenate([displacement_now, stiffness[None]], axis=0))
            padded_stiffness = extended[3]
        else:
            extended = extend(displacement_now)
        stretches, coupling = pl.pallas_call(
            stretch_kernel,
            out_shape=(
                jax.ShapeDtypeStruct((count,) + tuple(cell_shape), f32),
                jax.ShapeDtypeStruct(tuple(cell_shape), f32),
            ),
            grid=(cells_x // ROWS,),
            in_specs=[
                whole((3, halo_x, cells_y + 6, cells_z + 6)),
                bonds_spec,
                cells_spec,
                cells_spec,
            ],
            out_specs=(bonds_spec, cells_spec),
            scratch_shapes=[pltpu.VMEM((pairs, 3, halo_x, cells_y, cells_z), f32)],
            compiler_params=compiler_params(),
            interpret=INTERPRET,
        )(extended[:3], intact, weight, modulus_factor)
        padded_coupling = extended_2(coupling, (("gx", 0), ("gy", 1), ("gz", 2)), 3)
        displacement_now, velocity_now = pl.pallas_call(
            force_kernel,
            out_shape=(
                jax.ShapeDtypeStruct(displacement.shape, f32),
                jax.ShapeDtypeStruct(displacement.shape, f32),
            ),
            grid=(cells_x // ROWS,),
            in_specs=[
                whole((halo_x, cells_y + 6, cells_z + 6)),
                whole((halo_x, cells_y + 6, cells_z + 6)),
                bonds_spec,
                bonds_spec,
                vector_spec,
                vector_spec,
                vector_spec,
            ],
            out_specs=(vector_spec, vector_spec),
            scratch_shapes=[
                pltpu.VMEM((pairs, halo_x, cells_y, cells_z), f32),
                pltpu.VMEM((pairs, halo_x, cells_y, cells_z), f32),
            ],
            compiler_params=compiler_params(),
            interpret=INTERPRET,
        )(padded_coupling, padded_stiffness, stretches, intact, displacement_now, velocity_now, load_force)
    return (displacement_now, velocity_now)


def solution(mesh):
    placed = (
        P(None, "gx", "gy", "gz"),
        P(None, "gx", "gy", "gz"),
        P("gx", "gy", "gz"),
        P("gx", "gy", "gz"),
        P(None, "gx", "gy", "gz"),
        P("gx", "gy", "gz"),
        P(None, "gx", "gy", "gz"),
    )
    return jax.shard_map(
        local,
        mesh=mesh,
        in_specs=placed,
        out_specs=(P(None, "gx", "gy", "gz"), P(None, "gx", "gy", "gz")),
        check_vma=False,
    )
```

profile of v0, /device:TPU:106, one launch (start us, length us, event | category | flops | bytes accessed | tf_op | source)
XLA Modules:
  0.0 221.6 jit_solution(8874927244140914357)
XLA Ops:
  4.4 6.3 %multiply_multiply_fusion = (f32[122,16,8,128]{3,2,1,0:T(8,128)}, f32[16,8,128]{2,1,0:T(8,128)S(1)}) fusion(s32[128,16,8,128]{3,2,1,0:T(8,128)S(1)} %bitcast.26, s32[122]{0:T(128)S(1)} %bitcast.55, f32[122,128]{1,0:T(8,128)S(1)} %stack.20, f32[122,16,8]{2,1,0:T(8,128)S(1)} %broadcast_multiply_fusion, f32[122]{0:T(128)S(1)} %copy-done.9), kind=kLoop, calls=%fused_computation | loop fusion | flops 15974400 | bytes 16182224 | tf_op jit(solution)/shard_map/mul | solution.py:166
  13.4 5.0 %collective-permute-start = (f32[12288]{0:T(1024)S(1)}, f32[12288]{0:T(1024)S(1)}, u32[]{:S(2)}, u32[]{:S(2)}) collective-permute-start(f32[12288]{0:T(1024)S(1)} %bitcast.51), channel_id=1, source_target_pairs={{0,32},{32,64},{64,96},{96,128},{128,160},{160,192},{192,224},{1,3... | collective-permute-start | bytes 147464 | tf_op jit(solution)/shard_map/ppermute | solution.py:28
  22.3 2.4 %collective-permute-start.2 = (f32[33792]{0:T(1024)S(1)}, f32[33792]{0:T(1024)S(1)}, u32[]{:S(2)}, u32[]{:S(2)}) collective-permute-start(f32[33792]{0:T(1024)S(1)} %reshape.512), channel_id=1, source_target_pairs={{0,8},{8,16},{16,24},{1,9},{9,17},{17,25},{2,10},{10,18},{18,26},{... | collective-permute-start | bytes 405512 | tf_op jit(solution)/shard_map/ppermute | solution.py:28
  24.8 3.8 %collective-permute-done.2 = f32[33792]{0:T(1024)S(1)} collective-permute-done((f32[33792]{0:T(1024)S(1)}, f32[33792]{0:T(1024)S(1)}, u32[]{:S(2)}, u32[]{:S(2)}) %collective-permute-start.2) | collective-permute-done | bytes 135200 | tf_op jit(solution)/shard_map/ppermute | solution.py:28
  29.4 4.0 %collective-permute-start.4 = (f32[3696]{0:T(1024)S(1)}, f32[3696]{0:T(1024)S(1)}, u32[]{:S(2)}, u32[]{:S(2)}) collective-permute-start(f32[3696]{0:T(1024)S(1)} %reshape.516), channel_id=1, source_target_pairs={{0,1},{1,2},{2,3},{3,4},{4,5},{5,6},{6,7},{8,9},{9,10},{10,11},{11... | collective-permute-start | bytes 44360 | tf_op jit(solution)/shard_map/ppermute | solution.py:28
  33.8 4.2 %collective-permute-start.5 = (f32[3696]{0:T(1024)S(1)}, f32[3696]{0:T(1024)S(1)}, u32[]{:S(2)}, u32[]{:S(2)}) collective-permute-start(f32[3696]{0:T(1024)S(1)} %reshape.518), channel_id=1, source_target_pairs={{1,0},{2,1},{3,2},{4,3},{5,4},{6,5},{7,6},{9,8},{10,9},{11,10},{12... | collective-permute-start | bytes 44360 | tf_op jit(solution)/shard_map/ppermute | solution.py:30
  38.4 2.6 %collective-permute-done.5 = f32[3696]{0:T(1024)S(1)} collective-permute-done((f32[3696]{0:T(1024)S(1)}, f32[3696]{0:T(1024)S(1)}, u32[]{:S(2)}, u32[]{:S(2)}) %collective-permute-start.5) | collective-permute-done | bytes 14816 | tf_op jit(solution)/shard_map/ppermute | solution.py:30
  44.4 19.1 %shard_map.95 = (f32[122,16,8,128]{3,2,1,0:T(8,128)}, f32[16,8,128]{2,1,0:T(8,128)}) custom-call(f32[3,22,14,134]{3,2,1,0:T(8,128)} %slice.112.ext_ref, f32[122,16,8,128]{3,2,1,0:T(8,128)} %get-tuple-element.14.intact_ref, f32[16,8,128]{2,1,0:T(8,128)} %copy-done.3, f32[16,8,128]{2,1,0:T(8,128)} %get-tuple-element.40.factor_ref), custom_call_target="tpu_custom_call" | custom-call | tf_op jit(solution)/shard_map/pallas_call | solution.py:189
  64.2 5.4 %collective-permute-start.6 = (f32[3072]{0:T(1024)S(1)}, f32[3072]{0:T(1024)S(1)}, u32[]{:S(2)}, u32[]{:S(2)}) collective-permute-start(f32[3072]{0:T(1024)S(1)} %get-tuple-element.38), channel_id=1, source_target_pairs={{0,32},{32,64},{64,96},{96,128},{128,160},{160,192},{192,224},{1,3... | collective-permute-start | bytes 36872 | tf_op jit(solution)/shard_map/ppermute | solution.py:28
  72.5 4.0 %collective-permute-done.7 = f32[3072]{0:T(1024)S(1)} collective-permute-done((f32[3072]{0:T(1024)S(1)}, f32[3072]{0:T(1024)S(1)}, u32[]{:S(2)}, u32[]{:S(2)}) %collective-permute-start.7) | collective-permute-done | bytes 12320 | tf_op jit(solution)/shard_map/ppermute | solution.py:30
  86.0 5.1 %collective-permute-start.11 = (f32[924]{0:T(1024)S(1)}, f32[924]{0:T(1024)S(1)}, u32[]{:S(2)}, u32[]{:S(2)}) collective-permute-start(f32[924]{0:T(1024)S(1)} %reshape.530), channel_id=1, source_target_pairs={{1,0},{2,1},{3,2},{4,3},{5,4},{6,5},{7,6},{9,8},{10,9},{11,10},{12... | collective-permute-start | bytes 11096 | tf_op jit(solution)/shard_map/ppermute | solution.py:30
  95.1 3.9 %collective-permute-done.10 = f32[924]{0:T(1024)S(1)} collective-permute-done((f32[924]{0:T(1024)S(1)}, f32[924]{0:T(1024)S(1)}, u32[]{:S(2)}, u32[]{:S(2)}) %collective-permute-start.10) | collective-permute-done | bytes 3728 | tf_op jit(solution)/shard_map/ppermute | solution.py:28
  100.5 16.8 %shard_map.96 = (f32[3,16,8,128]{3,2,1,0:T(8,128)}, f32[3,16,8,128]{3,2,1,0:T(8,128)}) custom-call(f32[22,14,134]{2,1,0:T(8,128)} %pad_maximum_fusion.5.pc_ref, f32[22,14,134]{2,1,0:T(8,128)} %slice_bitcast_fusion.ps_ref, f32[122,16,8,128]{3,2,1,0:T(8,128)} %get-tuple-element.9.stretch_ref, f32[122,16,8,128]{3,2,1,0:T(8,128)} %get-tuple-element.14.intact_ref, ...), custom_call_target="tpu_custom_call" | custom-call | tf_op jit(solution)/shard_map/pallas_call | solution.py:208
  120.1 5.1 %collective-permute-start.12 = (f32[9216]{0:T(1024)S(1)}, f32[9216]{0:T(1024)S(1)}, u32[]{:S(2)}, u32[]{:S(2)}) collective-permute-start(f32[9216]{0:T(1024)S(1)} %bitcast.53), channel_id=1, source_target_pairs={{0,32},{32,64},{64,96},{96,128},{128,160},{160,192},{192,224},{1,3... | collective-permute-start | bytes 110600 | tf_op jit(solution)/shard_map/ppermute | solution.py:28
  129.9 2.6 %collective-permute-start.14 = (f32[25344]{0:T(1024)S(1)}, f32[25344]{0:T(1024)S(1)}, u32[]{:S(2)}, u32[]{:S(2)}) collective-permute-start(f32[25344]{0:T(1024)S(1)} %reshape.536), channel_id=1, source_target_pairs={{0,8},{8,16},{16,24},{1,9},{9,17},{17,25},{2,10},{10,18},{18,26},{... | collective-permute-start | bytes 304136 | tf_op jit(solution)/shard_map/ppermute | solution.py:28
  132.5 3.3 %collective-permute-done.14 = f32[25344]{0:T(1024)S(1)} collective-permute-done((f32[25344]{0:T(1024)S(1)}, f32[25344]{0:T(1024)S(1)}, u32[]{:S(2)}, u32[]{:S(2)}) %collective-permute-start.14) | collective-permute-done | bytes 101408 | tf_op jit(solution)/shard_map/ppermute | solution.py:28
  138.8 6.0 %collective-permute-start.17 = (f32[2772]{0:T(1024)S(1)}, f32[2772]{0:T(1024)S(1)}, u32[]{:S(2)}, u32[]{:S(2)}) collective-permute-start(f32[2772]{0:T(1024)S(1)} %reshape.542), channel_id=1, source_target_pairs={{1,0},{2,1},{3,2},{4,3},{5,4},{6,5},{7,6},{9,8},{10,9},{11,10},{12... | collective-permute-start | bytes 33272 | tf_op jit(solution)/shard_map/ppermute | solution.py:30
  148.6 19.0 %shard_map.97 = (f32[122,16,8,128]{3,2,1,0:T(8,128)}, f32[16,8,128]{2,1,0:T(8,128)}) custom-call(f32[3,22,14,134]{3,2,1,0:T(8,128)} %pad_maximum_fusion.1.ext_ref, f32[122,16,8,128]{3,2,1,0:T(8,128)} %get-tuple-element.14.intact_ref, f32[16,8,128]{2,1,0:T(8,128)} %copy-done.3, f32[16,8,128]{2,1,0:T(8,128)} %get-tuple-element.40.factor_ref), custom_call_target="tpu_custom_call" | custom-call | tf_op jit(solution)/shard_map/pallas_call | solution.py:189
  168.5 5.5 %collective-permute-start.18 = (f32[3072]{0:T(1024)S(1)}, f32[3072]{0:T(1024)S(1)}, u32[]{:S(2)}, u32[]{:S(2)}) collective-permute-start(f32[3072]{0:T(1024)S(1)} %get-tuple-element.36), channel_id=1, source_target_pairs={{0,32},{32,64},{64,96},{96,128},{128,160},{160,192},{192,224},{1,3... | collective-permute-start | bytes 36872 | tf_op jit(solution)/shard_map/ppermute | solution.py:28
  175.9 4.9 %collective-permute-done.19 = f32[3072]{0:T(1024)S(1)} collective-permute-done((f32[3072]{0:T(1024)S(1)}, f32[3072]{0:T(1024)S(1)}, u32[]{:S(2)}, u32[]{:S(2)}) %collective-permute-start.19) | collective-permute-done | bytes 12320 | tf_op jit(solution)/shard_map/ppermute | solution.py:30
  186.0 2.8 %collective-permute-done.20 = f32[8448]{0:T(1024)S(1)} collective-permute-done((f32[8448]{0:T(1024)S(1)}, f32[8448]{0:T(1024)S(1)}, u32[]{:S(2)}, u32[]{:S(2)}) %collective-permute-start.20) | collective-permute-done | bytes 33824 | tf_op jit(solution)/shard_map/ppermute | solution.py:28
  190.1 6.3 %collective-permute-start.22 = (f32[924]{0:T(1024)S(1)}, f32[924]{0:T(1024)S(1)}, u32[]{:S(2)}, u32[]{:S(2)}) collective-permute-start(f32[924]{0:T(1024)S(1)} %reshape.552), channel_id=1, source_target_pairs={{0,1},{1,2},{2,3},{3,4},{4,5},{5,6},{6,7},{8,9},{9,10},{10,11},{11... | collective-permute-start | bytes 11096 | tf_op jit(solution)/shard_map/ppermute | solution.py:28
  198.8 4.9 %collective-permute-done.23 = f32[924]{0:T(1024)S(1)} collective-permute-done((f32[924]{0:T(1024)S(1)}, f32[924]{0:T(1024)S(1)}, u32[]{:S(2)}, u32[]{:S(2)}) %collective-permute-start.23) | collective-permute-done | bytes 3728 | tf_op jit(solution)/shard_map/ppermute | solution.py:30
  204.9 16.7 %shard_map.98 = (f32[3,16,8,128]{3,2,1,0:T(8,128)}, f32[3,16,8,128]{3,2,1,0:T(8,128)}) custom-call(f32[22,14,134]{2,1,0:T(8,128)} %pad_maximum_fusion.6.pc_ref, f32[22,14,134]{2,1,0:T(8,128)} %slice_bitcast_fusion.ps_ref, f32[122,16,8,128]{3,2,1,0:T(8,128)} %get-tuple-element.12.stretch_ref, f32[122,16,8,128]{3,2,1,0:T(8,128)} %get-tuple-element.14.intact_ref, ...), custom_call_target="tpu_custom_call" | custom-call | tf_op jit(solution)/shard_map/pallas_call | solution.py:208
  (141 shorter events, 60.4 us)
Async XLA Ops:
  11.3 7.2 %collective-permute-start.1 = (f32[12288]{0:T(1024)S(1)}, f32[12288]{0:T(1024)S(1)}, u32[]{:S(2)}, u32[]{:S(2)}) collective-permute-start(f32[12288]{0:T(1024)S(1)} %bitcast.52), channel_id=1, source_target_pairs={{32,0},{64,32},{96,64},{128,96},{160,128},{192,160},{224,192},{33,... | collective-permute-start | bytes 147464 | tf_op jit(solution)/shard_map/ppermute | solution.py:30
  13.4 6.8 %collective-permute-start = (f32[12288]{0:T(1024)S(1)}, f32[12288]{0:T(1024)S(1)}, u32[]{:S(2)}, u32[]{:S(2)}) collective-permute-start(f32[12288]{0:T(1024)S(1)} %bitcast.51), channel_id=1, source_target_pairs={{0,32},{32,64},{64,96},{96,128},{128,160},{160,192},{192,224},{1,3... | collective-permute-start | bytes 147464 | tf_op jit(solution)/shard_map/ppermute | solution.py:28
  20.3 4.5 %collective-permute-start.3 = (f32[33792]{0:T(1024)S(1)}, f32[33792]{0:T(1024)S(1)}, u32[]{:S(2)}, u32[]{:S(2)}) collective-permute-start(f32[33792]{0:T(1024)S(1)} %reshape.514), channel_id=1, source_target_pairs={{8,0},{16,8},{24,16},{9,1},{17,9},{25,17},{10,2},{18,10},{26,18},{... | collective-permute-start | bytes 405512 | tf_op jit(solution)/shard_map/ppermute | solution.py:30
  22.3 6.3 %collective-permute-start.2 = (f32[33792]{0:T(1024)S(1)}, f32[33792]{0:T(1024)S(1)}, u32[]{:S(2)}, u32[]{:S(2)}) collective-permute-start(f32[33792]{0:T(1024)S(1)} %reshape.512), channel_id=1, source_target_pairs={{0,8},{8,16},{16,24},{1,9},{9,17},{17,25},{2,10},{10,18},{18,26},{... | collective-permute-start | bytes 405512 | tf_op jit(solution)/shard_map/ppermute | solution.py:28
  29.4 8.6 %collective-permute-start.4 = (f32[3696]{0:T(1024)S(1)}, f32[3696]{0:T(1024)S(1)}, u32[]{:S(2)}, u32[]{:S(2)}) collective-permute-start(f32[3696]{0:T(1024)S(1)} %reshape.516), channel_id=1, source_target_pairs={{0,1},{1,2},{2,3},{3,4},{4,5},{5,6},{6,7},{8,9},{9,10},{10,11},{11... | collective-permute-start | bytes 44360 | tf_op jit(solution)/shard_map/ppermute | solution.py:28
  33.8 7.1 %collective-permute-start.5 = (f32[3696]{0:T(1024)S(1)}, f32[3696]{0:T(1024)S(1)}, u32[]{:S(2)}, u32[]{:S(2)}) collective-permute-start(f32[3696]{0:T(1024)S(1)} %reshape.518), channel_id=1, source_target_pairs={{1,0},{2,1},{3,2},{4,3},{5,4},{6,5},{7,6},{9,8},{10,9},{11,10},{12... | collective-permute-start | bytes 44360 | tf_op jit(solution)/shard_map/ppermute | solution.py:30
  64.2 8.2 %collective-permute-start.6 = (f32[3072]{0:T(1024)S(1)}, f32[3072]{0:T(1024)S(1)}, u32[]{:S(2)}, u32[]{:S(2)}) collective-permute-start(f32[3072]{0:T(1024)S(1)} %get-tuple-element.38), channel_id=1, source_target_pairs={{0,32},{32,64},{64,96},{96,128},{128,160},{160,192},{192,224},{1,3... | collective-permute-start | bytes 36872 | tf_op jit(solution)/shard_map/ppermute | solution.py:28
  69.7 6.8 %collective-permute-start.7 = (f32[3072]{0:T(1024)S(1)}, f32[3072]{0:T(1024)S(1)}, u32[]{:S(2)}, u32[]{:S(2)}) collective-permute-start(f32[3072]{0:T(1024)S(1)} %get-tuple-element.39), channel_id=1, source_target_pairs={{32,0},{64,32},{96,64},{128,96},{160,128},{192,160},{224,192},{33,... | collective-permute-start | bytes 36872 | tf_op jit(solution)/shard_map/ppermute | solution.py:30
  77.4 6.0 %collective-permute-start.9 = (f32[8448]{0:T(1024)S(1)}, f32[8448]{0:T(1024)S(1)}, u32[]{:S(2)}, u32[]{:S(2)}) collective-permute-start(f32[8448]{0:T(1024)S(1)} %reshape.526), channel_id=1, source_target_pairs={{8,0},{16,8},{24,16},{9,1},{17,9},{25,17},{10,2},{18,10},{26,18},{... | collective-permute-start | bytes 101384 | tf_op jit(solution)/shard_map/ppermute | solution.py:30
  79.3 5.3 %collective-permute-start.8 = (f32[8448]{0:T(1024)S(1)}, f32[8448]{0:T(1024)S(1)}, u32[]{:S(2)}, u32[]{:S(2)}) collective-permute-start(f32[8448]{0:T(1024)S(1)} %reshape.524), channel_id=1, source_target_pairs={{0,8},{8,16},{16,24},{1,9},{9,17},{17,25},{2,10},{10,18},{18,26},{... | collective-permute-start | bytes 101384 | tf_op jit(solution)/shard_map/ppermute | solution.py:28
  86.0 13.2 %collective-permute-start.11 = (f32[924]{0:T(1024)S(1)}, f32[924]{0:T(1024)S(1)}, u32[]{:S(2)}, u32[]{:S(2)}) collective-permute-start(f32[924]{0:T(1024)S(1)} %reshape.530), channel_id=1, source_target_pairs={{1,0},{2,1},{3,2},{4,3},{5,4},{6,5},{7,6},{9,8},{10,9},{11,10},{12... | collective-permute-start | bytes 11096 | tf_op jit(solution)/shard_map/ppermute | solution.py:30
  91.2 7.9 %collective-permute-start.10 = (f32[924]{0:T(1024)S(1)}, f32[924]{0:T(1024)S(1)}, u32[]{:S(2)}, u32[]{:S(2)}) collective-permute-start(f32[924]{0:T(1024)S(1)} %reshape.528), channel_id=1, source_target_pairs={{0,1},{1,2},{2,3},{3,4},{4,5},{5,6},{6,7},{8,9},{9,10},{10,11},{11... | collective-permute-start | bytes 11096 | tf_op jit(solution)/shard_map/ppermute | solution.py:28
  118.1 7.1 %collective-permute-start.13 = (f32[9216]{0:T(1024)S(1)}, f32[9216]{0:T(1024)S(1)}, u32[]{:S(2)}, u32[]{:S(2)}) collective-permute-start(f32[9216]{0:T(1024)S(1)} %bitcast.54), channel_id=1, source_target_pairs={{32,0},{64,32},{96,64},{128,96},{160,128},{192,160},{224,192},{33,... | collective-permute-start | bytes 110600 | tf_op jit(solution)/shard_map/ppermute | solution.py:30
  120.1 6.8 %collective-permute-start.12 = (f32[9216]{0:T(1024)S(1)}, f32[9216]{0:T(1024)S(1)}, u32[]{:S(2)}, u32[]{:S(2)}) collective-permute-start(f32[9216]{0:T(1024)S(1)} %bitcast.53), channel_id=1, source_target_pairs={{0,32},{32,64},{64,96},{96,128},{128,160},{160,192},{192,224},{1,3... | collective-permute-start | bytes 110600 | tf_op jit(solution)/shard_map/ppermute | solution.py:28
  127.9 4.6 %collective-permute-start.15 = (f32[25344]{0:T(1024)S(1)}, f32[25344]{0:T(1024)S(1)}, u32[]{:S(2)}, u32[]{:S(2)}) collective-permute-start(f32[25344]{0:T(1024)S(1)} %reshape.538), channel_id=1, source_target_pairs={{8,0},{16,8},{24,16},{9,1},{17,9},{25,17},{10,2},{18,10},{26,18},{... | collective-permute-start | bytes 304136 | tf_op jit(solution)/shard_map/ppermute | solution.py:30
  129.9 6.0 %collective-permute-start.14 = (f32[25344]{0:T(1024)S(1)}, f32[25344]{0:T(1024)S(1)}, u32[]{:S(2)}, u32[]{:S(2)}) collective-permute-start(f32[25344]{0:T(1024)S(1)} %reshape.536), channel_id=1, source_target_pairs={{0,8},{8,16},{16,24},{1,9},{9,17},{17,25},{2,10},{10,18},{18,26},{... | collective-permute-start | bytes 304136 | tf_op jit(solution)/shard_map/ppermute | solution.py:28
  136.4 8.5 %collective-permute-start.16 = (f32[2772]{0:T(1024)S(1)}, f32[2772]{0:T(1024)S(1)}, u32[]{:S(2)}, u32[]{:S(2)}) collective-permute-start(f32[2772]{0:T(1024)S(1)} %reshape.540), channel_id=1, source_target_pairs={{0,1},{1,2},{2,3},{3,4},{4,5},{5,6},{6,7},{8,9},{9,10},{10,11},{11... | collective-permute-start | bytes 33272 | tf_op jit(solution)/shard_map/ppermute | solution.py:28
  138.8 7.8 %collective-permute-start.17 = (f32[2772]{0:T(1024)S(1)}, f32[2772]{0:T(1024)S(1)}, u32[]{:S(2)}, u32[]{:S(2)}) collective-permute-start(f32[2772]{0:T(1024)S(1)} %reshape.542), channel_id=1, source_target_pairs={{1,0},{2,1},{3,2},{4,3},{5,4},{6,5},{7,6},{9,8},{10,9},{11,10},{12... | collective-permute-start | bytes 33272 | tf_op jit(solution)/shard_map/ppermute | solution.py:30
  168.5 7.4 %collective-permute-start.18 = (f32[3072]{0:T(1024)S(1)}, f32[3072]{0:T(1024)S(1)}, u32[]{:S(2)}, u32[]{:S(2)}) collective-permute-start(f32[3072]{0:T(1024)S(1)} %get-tuple-element.36), channel_id=1, source_target_pairs={{0,32},{32,64},{64,96},{96,128},{128,160},{160,192},{192,224},{1,3... | collective-permute-start | bytes 36872 | tf_op jit(solution)/shard_map/ppermute | solution.py:28
  173.9 6.8 %collective-permute-start.19 = (f32[3072]{0:T(1024)S(1)}, f32[3072]{0:T(1024)S(1)}, u32[]{:S(2)}, u32[]{:S(2)}) collective-permute-start(f32[3072]{0:T(1024)S(1)} %get-tuple-element.37), channel_id=1, source_target_pairs={{32,0},{64,32},{96,64},{128,96},{160,128},{192,160},{224,192},{33,... | collective-permute-start | bytes 36872 | tf_op jit(solution)/shard_map/ppermute | solution.py:30
  181.6 4.4 %collective-permute-start.21 = (f32[8448]{0:T(1024)S(1)}, f32[8448]{0:T(1024)S(1)}, u32[]{:S(2)}, u32[]{:S(2)}) collective-permute-start(f32[8448]{0:T(1024)S(1)} %reshape.550), channel_id=1, source_target_pairs={{8,0},{16,8},{24,16},{9,1},{17,9},{25,17},{10,2},{18,10},{26,18},{... | collective-permute-start | bytes 101384 | tf_op jit(solution)/shard_map/ppermute | solution.py:30
  183.6 5.3 %collective-permute-start.20 = (f32[8448]{0:T(1024)S(1)}, f32[8448]{0:T(1024)S(1)}, u32[]{:S(2)}, u32[]{:S(2)}) collective-permute-start(f32[8448]{0:T(1024)S(1)} %reshape.548), channel_id=1, source_target_pairs={{0,8},{8,16},{16,24},{1,9},{9,17},{17,25},{2,10},{10,18},{18,26},{... | collective-permute-start | bytes 101384 | tf_op jit(solution)/shard_map/ppermute | solution.py:28
  190.1 8.5 %collective-permute-start.22 = (f32[924]{0:T(1024)S(1)}, f32[924]{0:T(1024)S(1)}, u32[]{:S(2)}, u32[]{:S(2)}) collective-permute-start(f32[924]{0:T(1024)S(1)} %reshape.552), channel_id=1, source_target_pairs={{0,1},{1,2},{2,3},{3,4},{4,5},{5,6},{6,7},{8,9},{9,10},{10,11},{11... | collective-permute-start | bytes 11096 | tf_op jit(solution)/shard_map/ppermute | solution.py:28
  196.6 7.0 %collective-permute-start.23 = (f32[924]{0:T(1024)S(1)}, f32[924]{0:T(1024)S(1)}, u32[]{:S(2)}, u32[]{:S(2)}) collective-permute-start(f32[924]{0:T(1024)S(1)} %reshape.554), channel_id=1, source_target_pairs={{1,0},{2,1},{3,2},{4,3},{5,4},{6,5},{7,6},{9,8},{10,9},{11,10},{12... | collective-permute-start | bytes 11096 | tf_op jit(solution)/shard_map/ppermute | solution.py:30
  (10 other events, 104.7 us)
where the time goes:
time: 223 us; the launch traced here: 222 us
  starting transfers between devices  78.4 us (35%)
  Pallas kernels  71.6 us (32%)
  waiting for transfers between devices  36.4 us (16%)
  other arithmetic  19.4 us (9%)
  local copies, waits for them, and re-layouts  14.5 us (7%)
    ppermute x12, starting transfers between devices, extended_2(): lax.ppermute(tail.reshape(-1), axis, [(i, (i + 1) % count) for i in range...  45.7 us
    pallas_call x2, Pallas kernels, local(): pl.pallas_call(stretch_kernel, out_shape=(jax.ShapeDtypeStruct((count,) +...  38.1 us
    pallas_call x2, Pallas kernels, local(): pl.pallas_call(force_kernel, out_shape=(jax.ShapeDtypeStruct(displacement...  33.5 us
    ppermute x12, starting transfers between devices, extended_2(): lax.ppermute(head.reshape(-1), axis, [((i + 1) % count, i) for i in range...  32.7 us
    ppermute x12, waiting for transfers between devices, extended_2(): lax.ppermute(tail.reshape(-1), axis, [(i, (i + 1) % count) for i in range...  18.3 us
    ppermute x12, waiting for transfers between devices, extended_2(): lax.ppermute(head.reshape(-1), axis, [((i + 1) % count, i) for i in range...  18 us
    concatenate x12, other arithmetic, extended_2(): jnp.concatenate([lax.ppermute(tail.reshape(-1), axis, [(i, (i + 1) % coun...  9.51 us
    mul x1, other arithmetic, local(): intact = exists * (1.0 - bits.astype(jnp.float32))  6.26 us
  transfers between devices with their start and end apart: 24, of which 13 were waited for; matrix products, arithmetic and copies ran while one was open for 3% of the time, Pallas kernels for 0%

commit v1 on v0

--- a/solution.py
+++ b/solution.py
@@ -68,16 +68,19 @@
 
 def fill_stack(stack_ref, padded_ref, leading):
     cells_y, cells_z = stack_ref.shape[-2], stack_ref.shape[-1]
-
-    def row(index, carry):
+    trips = 2
+    chunk = stack_ref.shape[-3] // trips
+
+    def rows(trip, carry):
+        start = trip * chunk
         for pair, (oy, oz) in enumerate(PAIRS):
             for c in leading:
-                target = (pair, pl.ds(index, 1)) if c is None else (pair, c, pl.ds(index, 1))
-                source = (pl.ds(index, 1),) if c is None else (c, pl.ds(index, 1))
+                target = (pair, pl.ds(start, chunk)) if c is None else (pair, c, pl.ds(start, chunk))
+                source = (pl.ds(start, chunk),) if c is None else (c, pl.ds(start, chunk))
                 stack_ref[target] = padded_ref[source + (pl.ds(3 + oy, cells_y), pl.ds(3 + oz, cells_z))]
         return carry
 
-    lax.fori_loop(0, stack_ref.shape[-3], row, 0)
+    lax.fori_loop(0, trips, rows, 0)
 
 
 def stretch_kernel(ext_ref, intact_ref, weight_ref, factor_ref, stretch_ref, coupling_ref, us_ref):

time: 223 us -> 215 us (0.964)
  Pallas kernels: 71.6 us -> 63.4 us
    pallas_call x2, Pallas kernels: 33.5 us -> 28.1 us  [local(): pl.pallas_call(force_kernel, out_shape=(jax.ShapeDtypeStruct(displacement...]
    pallas_call x2, Pallas kernels: 38.1 us -> 35.4 us  [local(): pl.pallas_call(stretch_kernel, out_shape=(jax.ShapeDtypeStruct((count,) +...]
where the time goes in v1:
time: 215 us; the launch traced here: 214 us
  starting transfers between devices  78.9 us (37%)
  Pallas kernels  63.4 us (29%)
  waiting for transfers between devices  36.1 us (17%)
  other arithmetic  19.4 us (9%)
  local copies, waits for them, and re-layouts  14.5 us (7%)
    ppermute x12, starting transfers between devices, extended_2(): lax.ppermute(tail.reshape(-1), axis, [(i, (i + 1) % count) for i in range...  45.5 us
    pallas_call x2, Pallas kernels, local(): pl.pallas_call(stretch_kernel, out_shape=(jax.ShapeDtypeStruct((count,) +...  35.4 us
    ppermute x12, starting transfers between devices, extended_2(): lax.ppermute(head.reshape(-1), axis, [((i + 1) % count, i) for i in range...  33.4 us
    pallas_call x2, Pallas kernels, local(): pl.pallas_call(force_kernel, out_shape=(jax.ShapeDtypeStruct(displacement...  28.1 us
    ppermute x12, waiting for transfers between devices, extended_2(): lax.ppermute(tail.reshape(-1), axis, [(i, (i + 1) % count) for i in range...  18.5 us
    ppermute x12, waiting for transfers between devices, extended_2(): lax.ppermute(head.reshape(-1), axis, [((i + 1) % count, i) for i in range...  17.6 us
    concatenate x12, other arithmetic, extended_2(): jnp.concatenate([lax.ppermute(tail.reshape(-1), axis, [(i, (i + 1) % coun...  9.51 us
    mul x1, other arithmetic, local(): intact = exists * (1.0 - bits.astype(jnp.float32))  6.26 us
  transfers between devices with their start and end apart: 24, of which 13 were waited for; matrix products, arithmetic and copies ran while one was open for 3% of the time, Pallas kernels for 0%

profile of v1, /device:TPU:106, one launch (start us, length us, event | category | flops | bytes accessed | tf_op | source)
XLA Modules:
  0.0 213.7 jit_solution(17388583900711347294)
XLA Ops:
  4.4 6.3 %multiply_multiply_fusion = (f32[122,16,8,128]{3,2,1,0:T(8,128)}, f32[16,8,128]{2,1,0:T(8,128)S(1)}) fusion(s32[128,16,8,128]{3,2,1,0:T(8,128)S(1)} %bitcast.26, s32[122]{0:T(128)S(1)} %bitcast.55, f32[122,128]{1,0:T(8,128)S(1)} %stack.20, f32[122,16,8]{2,1,0:T(8,128)S(1)} %broadcast_multiply_fusion, f32[122]{0:T(128)S(1)} %copy-done.9), kind=kLoop, calls=%fused_computation | loop fusion | flops 15974400 | bytes 16182224 | tf_op jit(solution)/shard_map/mul | solution.py:169
  13.4 5.0 %collective-permute-start = (f32[12288]{0:T(1024)S(1)}, f32[12288]{0:T(1024)S(1)}, u32[]{:S(2)}, u32[]{:S(2)}) collective-permute-start(f32[12288]{0:T(1024)S(1)} %bitcast.51), channel_id=1, source_target_pairs={{0,32},{32,64},{64,96},{96,128},{128,160},{160,192},{192,224},{1,3... | collective-permute-start | bytes 147464 | tf_op jit(solution)/shard_map/ppermute | solution.py:28
  22.3 2.4 %collective-permute-start.2 = (f32[33792]{0:T(1024)S(1)}, f32[33792]{0:T(1024)S(1)}, u32[]{:S(2)}, u32[]{:S(2)}) collective-permute-start(f32[33792]{0:T(1024)S(1)} %reshape.512), channel_id=1, source_target_pairs={{0,8},{8,16},{16,24},{1,9},{9,17},{17,25},{2,10},{10,18},{18,26},{... | collective-permute-start | bytes 405512 | tf_op jit(solution)/shard_map/ppermute | solution.py:28
  24.8 3.8 %collective-permute-done.2 = f32[33792]{0:T(1024)S(1)} collective-permute-done((f32[33792]{0:T(1024)S(1)}, f32[33792]{0:T(1024)S(1)}, u32[]{:S(2)}, u32[]{:S(2)}) %collective-permute-start.2) | collective-permute-done | bytes 135200 | tf_op jit(solution)/shard_map/ppermute | solution.py:28
  29.4 4.0 %collective-permute-start.4 = (f32[3696]{0:T(1024)S(1)}, f32[3696]{0:T(1024)S(1)}, u32[]{:S(2)}, u32[]{:S(2)}) collective-permute-start(f32[3696]{0:T(1024)S(1)} %reshape.516), channel_id=1, source_target_pairs={{0,1},{1,2},{2,3},{3,4},{4,5},{5,6},{6,7},{8,9},{9,10},{10,11},{11... | collective-permute-start | bytes 44360 | tf_op jit(solution)/shard_map/ppermute | solution.py:28
  33.8 4.2 %collective-permute-start.5 = (f32[3696]{0:T(1024)S(1)}, f32[3696]{0:T(1024)S(1)}, u32[]{:S(2)}, u32[]{:S(2)}) collective-permute-start(f32[3696]{0:T(1024)S(1)} %reshape.518), channel_id=1, source_target_pairs={{1,0},{2,1},{3,2},{4,3},{5,4},{6,5},{7,6},{9,8},{10,9},{11,10},{12... | collective-permute-start | bytes 44360 | tf_op jit(solution)/shard_map/ppermute | solution.py:30
  38.4 2.6 %collective-permute-done.5 = f32[3696]{0:T(1024)S(1)} collective-permute-done((f32[3696]{0:T(1024)S(1)}, f32[3696]{0:T(1024)S(1)}, u32[]{:S(2)}, u32[]{:S(2)}) %collective-permute-start.5) | collective-permute-done | bytes 14816 | tf_op jit(solution)/shard_map/ppermute | solution.py:30
  44.5 17.7 %shard_map.95 = (f32[122,16,8,128]{3,2,1,0:T(8,128)}, f32[16,8,128]{2,1,0:T(8,128)}) custom-call(f32[3,22,14,134]{3,2,1,0:T(8,128)} %slice.112.ext_ref, f32[122,16,8,128]{3,2,1,0:T(8,128)} %get-tuple-element.14.intact_ref, f32[16,8,128]{2,1,0:T(8,128)} %copy-done.3, f32[16,8,128]{2,1,0:T(8,128)} %get-tuple-element.40.factor_ref), custom_call_target="tpu_custom_call" | custom-call | tf_op jit(solution)/shard_map/pallas_call | solution.py:192
  62.9 5.4 %collective-permute-start.6 = (f32[3072]{0:T(1024)S(1)}, f32[3072]{0:T(1024)S(1)}, u32[]{:S(2)}, u32[]{:S(2)}) collective-permute-start(f32[3072]{0:T(1024)S(1)} %get-tuple-element.38), channel_id=1, source_target_pairs={{0,32},{32,64},{64,96},{96,128},{128,160},{160,192},{192,224},{1,3... | collective-permute-start | bytes 36872 | tf_op jit(solution)/shard_map/ppermute | solution.py:28
  71.3 4.0 %collective-permute-done.7 = f32[3072]{0:T(1024)S(1)} collective-permute-done((f32[3072]{0:T(1024)S(1)}, f32[3072]{0:T(1024)S(1)}, u32[]{:S(2)}, u32[]{:S(2)}) %collective-permute-start.7) | collective-permute-done | bytes 12320 | tf_op jit(solution)/shard_map/ppermute | solution.py:30
  84.9 5.1 %collective-permute-start.11 = (f32[924]{0:T(1024)S(1)}, f32[924]{0:T(1024)S(1)}, u32[]{:S(2)}, u32[]{:S(2)}) collective-permute-start(f32[924]{0:T(1024)S(1)} %reshape.530), channel_id=1, source_target_pairs={{1,0},{2,1},{3,2},{4,3},{5,4},{6,5},{7,6},{9,8},{10,9},{11,10},{12... | collective-permute-start | bytes 11096 | tf_op jit(solution)/shard_map/ppermute | solution.py:30
  94.0 3.9 %collective-permute-done.10 = f32[924]{0:T(1024)S(1)} collective-permute-done((f32[924]{0:T(1024)S(1)}, f32[924]{0:T(1024)S(1)}, u32[]{:S(2)}, u32[]{:S(2)}) %collective-permute-start.10) | collective-permute-done | bytes 3728 | tf_op jit(solution)/shard_map/ppermute | solution.py:28
  99.3 14.1 %shard_map.96 = (f32[3,16,8,128]{3,2,1,0:T(8,128)}, f32[3,16,8,128]{3,2,1,0:T(8,128)}) custom-call(f32[22,14,134]{2,1,0:T(8,128)} %pad_maximum_fusion.5.pc_ref, f32[22,14,134]{2,1,0:T(8,128)} %slice_bitcast_fusion.ps_ref, f32[122,16,8,128]{3,2,1,0:T(8,128)} %get-tuple-element.9.stretch_ref, f32[122,16,8,128]{3,2,1,0:T(8,128)} %get-tuple-element.14.intact_ref, ...), custom_call_target="tpu_custom_call" | custom-call | tf_op jit(solution)/shard_map/pallas_call | solution.py:211
  116.2 5.1 %collective-permute-start.12 = (f32[9216]{0:T(1024)S(1)}, f32[9216]{0:T(1024)S(1)}, u32[]{:S(2)}, u32[]{:S(2)}) collective-permute-start(f32[9216]{0:T(1024)S(1)} %bitcast.53), channel_id=1, source_target_pairs={{0,32},{32,64},{64,96},{96,128},{128,160},{160,192},{192,224},{1,3... | collective-permute-start | bytes 110600 | tf_op jit(solution)/shard_map/ppermute | solution.py:28
  126.0 2.4 %collective-permute-start.14 = (f32[25344]{0:T(1024)S(1)}, f32[25344]{0:T(1024)S(1)}, u32[]{:S(2)}, u32[]{:S(2)}) collective-permute-start(f32[25344]{0:T(1024)S(1)} %reshape.536), channel_id=1, source_target_pairs={{0,8},{8,16},{16,24},{1,9},{9,17},{17,25},{2,10},{10,18},{18,26},{... | collective-permute-start | bytes 304136 | tf_op jit(solution)/shard_map/ppermute | solution.py:28
  128.4 3.5 %collective-permute-done.14 = f32[25344]{0:T(1024)S(1)} collective-permute-done((f32[25344]{0:T(1024)S(1)}, f32[25344]{0:T(1024)S(1)}, u32[]{:S(2)}, u32[]{:S(2)}) %collective-permute-start.14) | collective-permute-done | bytes 101408 | tf_op jit(solution)/shard_map/ppermute | solution.py:28
  134.9 6.2 %collective-permute-start.17 = (f32[2772]{0:T(1024)S(1)}, f32[2772]{0:T(1024)S(1)}, u32[]{:S(2)}, u32[]{:S(2)}) collective-permute-start(f32[2772]{0:T(1024)S(1)} %reshape.542), channel_id=1, source_target_pairs={{1,0},{2,1},{3,2},{4,3},{5,4},{6,5},{7,6},{9,8},{10,9},{11,10},{12... | collective-permute-start | bytes 33272 | tf_op jit(solution)/shard_map/ppermute | solution.py:30
  144.7 17.7 %shard_map.97 = (f32[122,16,8,128]{3,2,1,0:T(8,128)}, f32[16,8,128]{2,1,0:T(8,128)}) custom-call(f32[3,22,14,134]{3,2,1,0:T(8,128)} %pad_maximum_fusion.1.ext_ref, f32[122,16,8,128]{3,2,1,0:T(8,128)} %get-tuple-element.14.intact_ref, f32[16,8,128]{2,1,0:T(8,128)} %copy-done.3, f32[16,8,128]{2,1,0:T(8,128)} %get-tuple-element.40.factor_ref), custom_call_target="tpu_custom_call" | custom-call | tf_op jit(solution)/shard_map/pallas_call | solution.py:192
  163.2 5.5 %collective-permute-start.18 = (f32[3072]{0:T(1024)S(1)}, f32[3072]{0:T(1024)S(1)}, u32[]{:S(2)}, u32[]{:S(2)}) collective-permute-start(f32[3072]{0:T(1024)S(1)} %get-tuple-element.36), channel_id=1, source_target_pairs={{0,32},{32,64},{64,96},{96,128},{128,160},{160,192},{192,224},{1,3... | collective-permute-start | bytes 36872 | tf_op jit(solution)/shard_map/ppermute | solution.py:28
  170.6 4.9 %collective-permute-done.19 = f32[3072]{0:T(1024)S(1)} collective-permute-done((f32[3072]{0:T(1024)S(1)}, f32[3072]{0:T(1024)S(1)}, u32[]{:S(2)}, u32[]{:S(2)}) %collective-permute-start.19) | collective-permute-done | bytes 12320 | tf_op jit(solution)/shard_map/ppermute | solution.py:30
  180.8 2.8 %collective-permute-done.20 = f32[8448]{0:T(1024)S(1)} collective-permute-done((f32[8448]{0:T(1024)S(1)}, f32[8448]{0:T(1024)S(1)}, u32[]{:S(2)}, u32[]{:S(2)}) %collective-permute-start.20) | collective-permute-done | bytes 33824 | tf_op jit(solution)/shard_map/ppermute | solution.py:28
  184.8 6.3 %collective-permute-start.22 = (f32[924]{0:T(1024)S(1)}, f32[924]{0:T(1024)S(1)}, u32[]{:S(2)}, u32[]{:S(2)}) collective-permute-start(f32[924]{0:T(1024)S(1)} %reshape.552), channel_id=1, source_target_pairs={{0,1},{1,2},{2,3},{3,4},{4,5},{5,6},{6,7},{8,9},{9,10},{10,11},{11... | collective-permute-start | bytes 11096 | tf_op jit(solution)/shard_map/ppermute | solution.py:28
  193.8 4.6 %collective-permute-done.23 = f32[924]{0:T(1024)S(1)} collective-permute-done((f32[924]{0:T(1024)S(1)}, f32[924]{0:T(1024)S(1)}, u32[]{:S(2)}, u32[]{:S(2)}) %collective-permute-start.23) | collective-permute-done | bytes 3728 | tf_op jit(solution)/shard_map/ppermute | solution.py:30
  199.6 14.0 %shard_map.98 = (f32[3,16,8,128]{3,2,1,0:T(8,128)}, f32[3,16,8,128]{3,2,1,0:T(8,128)}) custom-call(f32[22,14,134]{2,1,0:T(8,128)} %pad_maximum_fusion.6.pc_ref, f32[22,14,134]{2,1,0:T(8,128)} %slice_bitcast_fusion.ps_ref, f32[122,16,8,128]{3,2,1,0:T(8,128)} %get-tuple-element.12.stretch_ref, f32[122,16,8,128]{3,2,1,0:T(8,128)} %get-tuple-element.14.intact_ref, ...), custom_call_target="tpu_custom_call" | custom-call | tf_op jit(solution)/shard_map/pallas_call | solution.py:211
  (141 shorter events, 60.6 us)
Async XLA Ops:
  11.3 7.2 %collective-permute-start.1 = (f32[12288]{0:T(1024)S(1)}, f32[12288]{0:T(1024)S(1)}, u32[]{:S(2)}, u32[]{:S(2)}) collective-permute-start(f32[12288]{0:T(1024)S(1)} %bitcast.52), channel_id=1, source_target_pairs={{32,0},{64,32},{96,64},{128,96},{160,128},{192,160},{224,192},{33,... | collective-permute-start | bytes 147464 | tf_op jit(solution)/shard_map/ppermute | solution.py:30
  13.4 6.8 %collective-permute-start = (f32[12288]{0:T(1024)S(1)}, f32[12288]{0:T(1024)S(1)}, u32[]{:S(2)}, u32[]{:S(2)}) collective-permute-start(f32[12288]{0:T(1024)S(1)} %bitcast.51), channel_id=1, source_target_pairs={{0,32},{32,64},{64,96},{96,128},{128,160},{160,192},{192,224},{1,3... | collective-permute-start | bytes 147464 | tf_op jit(solution)/shard_map/ppermute | solution.py:28
  20.3 4.5 %collective-permute-start.3 = (f32[33792]{0:T(1024)S(1)}, f32[33792]{0:T(1024)S(1)}, u32[]{:S(2)}, u32[]{:S(2)}) collective-permute-start(f32[33792]{0:T(1024)S(1)} %reshape.514), channel_id=1, source_target_pairs={{8,0},{16,8},{24,16},{9,1},{17,9},{25,17},{10,2},{18,10},{26,18},{... | collective-permute-start | bytes 405512 | tf_op jit(solution)/shard_map/ppermute | solution.py:30
  22.3 6.3 %collective-permute-start.2 = (f32[33792]{0:T(1024)S(1)}, f32[33792]{0:T(1024)S(1)}, u32[]{:S(2)}, u32[]{:S(2)}) collective-permute-start(f32[33792]{0:T(1024)S(1)} %reshape.512), channel_id=1, source_target_pairs={{0,8},{8,16},{16,24},{1,9},{9,17},{17,25},{2,10},{10,18},{18,26},{... | collective-permute-start | bytes 405512 | tf_op jit(solution)/shard_map/ppermute | solution.py:28
  29.4 8.6 %collective-permute-start.4 = (f32[3696]{0:T(1024)S(1)}, f32[3696]{0:T(1024)S(1)}, u32[]{:S(2)}, u32[]{:S(2)}) collective-permute-start(f32[3696]{0:T(1024)S(1)} %reshape.516), channel_id=1, source_target_pairs={{0,1},{1,2},{2,3},{3,4},{4,5},{5,6},{6,7},{8,9},{9,10},{10,11},{11... | collective-permute-start | bytes 44360 | tf_op jit(solution)/shard_map/ppermute | solution.py:28
  33.8 7.1 %collective-permute-start.5 = (f32[3696]{0:T(1024)S(1)}, f32[3696]{0:T(1024)S(1)}, u32[]{:S(2)}, u32[]{:S(2)}) collective-permute-start(f32[3696]{0:T(1024)S(1)} %reshape.518), channel_id=1, source_target_pairs={{1,0},{2,1},{3,2},{4,3},{5,4},{6,5},{7,6},{9,8},{10,9},{11,10},{12... | collective-permute-start | bytes 44360 | tf_op jit(solution)/shard_map/ppermute | solution.py:30
  62.9 8.4 %collective-permute-start.6 = (f32[3072]{0:T(1024)S(1)}, f32[3072]{0:T(1024)S(1)}, u32[]{:S(2)}, u32[]{:S(2)}) collective-permute-start(f32[3072]{0:T(1024)S(1)} %get-tuple-element.38), channel_id=1, source_target_pairs={{0,32},{32,64},{64,96},{96,128},{128,160},{160,192},{192,224},{1,3... | collective-permute-start | bytes 36872 | tf_op jit(solution)/shard_map/ppermute | solution.py:28
  68.3 7.0 %collective-permute-start.7 = (f32[3072]{0:T(1024)S(1)}, f32[3072]{0:T(1024)S(1)}, u32[]{:S(2)}, u32[]{:S(2)}) collective-permute-start(f32[3072]{0:T(1024)S(1)} %get-tuple-element.39), channel_id=1, source_target_pairs={{32,0},{64,32},{96,64},{128,96},{160,128},{192,160},{224,192},{33,... | collective-permute-start | bytes 36872 | tf_op jit(solution)/shard_map/ppermute | solution.py:30
  76.2 6.0 %collective-permute-start.9 = (f32[8448]{0:T(1024)S(1)}, f32[8448]{0:T(1024)S(1)}, u32[]{:S(2)}, u32[]{:S(2)}) collective-permute-start(f32[8448]{0:T(1024)S(1)} %reshape.526), channel_id=1, source_target_pairs={{8,0},{16,8},{24,16},{9,1},{17,9},{25,17},{10,2},{18,10},{26,18},{... | collective-permute-start | bytes 101384 | tf_op jit(solution)/shard_map/ppermute | solution.py:30
  78.2 5.3 %collective-permute-start.8 = (f32[8448]{0:T(1024)S(1)}, f32[8448]{0:T(1024)S(1)}, u32[]{:S(2)}, u32[]{:S(2)}) collective-permute-start(f32[8448]{0:T(1024)S(1)} %reshape.524), channel_id=1, source_target_pairs={{0,8},{8,16},{16,24},{1,9},{9,17},{17,25},{2,10},{10,18},{18,26},{... | collective-permute-start | bytes 101384 | tf_op jit(solution)/shard_map/ppermute | solution.py:28
  84.9 13.2 %collective-permute-start.11 = (f32[924]{0:T(1024)S(1)}, f32[924]{0:T(1024)S(1)}, u32[]{:S(2)}, u32[]{:S(2)}) collective-permute-start(f32[924]{0:T(1024)S(1)} %reshape.530), channel_id=1, source_target_pairs={{1,0},{2,1},{3,2},{4,3},{5,4},{6,5},{7,6},{9,8},{10,9},{11,10},{12... | collective-permute-start | bytes 11096 | tf_op jit(solution)/shard_map/ppermute | solution.py:30
  90.0 7.9 %collective-permute-start.10 = (f32[924]{0:T(1024)S(1)}, f32[924]{0:T(1024)S(1)}, u32[]{:S(2)}, u32[]{:S(2)}) collective-permute-start(f32[924]{0:T(1024)S(1)} %reshape.528), channel_id=1, source_target_pairs={{0,1},{1,2},{2,3},{3,4},{4,5},{5,6},{6,7},{8,9},{9,10},{10,11},{11... | collective-permute-start | bytes 11096 | tf_op jit(solution)/shard_map/ppermute | solution.py:28
  114.2 7.1 %collective-permute-start.13 = (f32[9216]{0:T(1024)S(1)}, f32[9216]{0:T(1024)S(1)}, u32[]{:S(2)}, u32[]{:S(2)}) collective-permute-start(f32[9216]{0:T(1024)S(1)} %bitcast.54), channel_id=1, source_target_pairs={{32,0},{64,32},{96,64},{128,96},{160,128},{192,160},{224,192},{33,... | collective-permute-start | bytes 110600 | tf_op jit(solution)/shard_map/ppermute | solution.py:30
  116.2 6.8 %collective-permute-start.12 = (f32[9216]{0:T(1024)S(1)}, f32[9216]{0:T(1024)S(1)}, u32[]{:S(2)}, u32[]{:S(2)}) collective-permute-start(f32[9216]{0:T(1024)S(1)} %bitcast.53), channel_id=1, source_target_pairs={{0,32},{32,64},{64,96},{96,128},{128,160},{160,192},{192,224},{1,3... | collective-permute-start | bytes 110600 | tf_op jit(solution)/shard_map/ppermute | solution.py:28
  124.0 4.4 %collective-permute-start.15 = (f32[25344]{0:T(1024)S(1)}, f32[25344]{0:T(1024)S(1)}, u32[]{:S(2)}, u32[]{:S(2)}) collective-permute-start(f32[25344]{0:T(1024)S(1)} %reshape.538), channel_id=1, source_target_pairs={{8,0},{16,8},{24,16},{9,1},{17,9},{25,17},{10,2},{18,10},{26,18},{... | collective-permute-start | bytes 304136 | tf_op jit(solution)/shard_map/ppermute | solution.py:30
  126.0 6.0 %collective-permute-start.14 = (f32[25344]{0:T(1024)S(1)}, f32[25344]{0:T(1024)S(1)}, u32[]{:S(2)}, u32[]{:S(2)}) collective-permute-start(f32[25344]{0:T(1024)S(1)} %reshape.536), channel_id=1, source_target_pairs={{0,8},{8,16},{16,24},{1,9},{9,17},{17,25},{2,10},{10,18},{18,26},{... | collective-permute-start | bytes 304136 | tf_op jit(solution)/shard_map/ppermute | solution.py:28
  132.5 8.7 %collective-permute-start.16 = (f32[2772]{0:T(1024)S(1)}, f32[2772]{0:T(1024)S(1)}, u32[]{:S(2)}, u32[]{:S(2)}) collective-permute-start(f32[2772]{0:T(1024)S(1)} %reshape.540), channel_id=1, source_target_pairs={{0,1},{1,2},{2,3},{3,4},{4,5},{5,6},{6,7},{8,9},{9,10},{10,11},{11... | collective-permute-start | bytes 33272 | tf_op jit(solution)/shard_map/ppermute | solution.py:28
  134.9 7.8 %collective-permute-start.17 = (f32[2772]{0:T(1024)S(1)}, f32[2772]{0:T(1024)S(1)}, u32[]{:S(2)}, u32[]{:S(2)}) collective-permute-start(f32[2772]{0:T(1024)S(1)} %reshape.542), channel_id=1, source_target_pairs={{1,0},{2,1},{3,2},{4,3},{5,4},{6,5},{7,6},{9,8},{10,9},{11,10},{12... | collective-permute-start | bytes 33272 | tf_op jit(solution)/shard_map/ppermute | solution.py:30
  163.2 7.4 %collective-permute-start.18 = (f32[3072]{0:T(1024)S(1)}, f32[3072]{0:T(1024)S(1)}, u32[]{:S(2)}, u32[]{:S(2)}) collective-permute-start(f32[3072]{0:T(1024)S(1)} %get-tuple-element.36), channel_id=1, source_target_pairs={{0,32},{32,64},{64,96},{96,128},{128,160},{160,192},{192,224},{1,3... | collective-permute-start | bytes 36872 | tf_op jit(solution)/shard_map/ppermute | solution.py:28
  168.7 6.8 %collective-permute-start.19 = (f32[3072]{0:T(1024)S(1)}, f32[3072]{0:T(1024)S(1)}, u32[]{:S(2)}, u32[]{:S(2)}) collective-permute-start(f32[3072]{0:T(1024)S(1)} %get-tuple-element.37), channel_id=1, source_target_pairs={{32,0},{64,32},{96,64},{128,96},{160,128},{192,160},{224,192},{33,... | collective-permute-start | bytes 36872 | tf_op jit(solution)/shard_map/ppermute | solution.py:30
  176.4 4.4 %collective-permute-start.21 = (f32[8448]{0:T(1024)S(1)}, f32[8448]{0:T(1024)S(1)}, u32[]{:S(2)}, u32[]{:S(2)}) collective-permute-start(f32[8448]{0:T(1024)S(1)} %reshape.550), channel_id=1, source_target_pairs={{8,0},{16,8},{24,16},{9,1},{17,9},{25,17},{10,2},{18,10},{26,18},{... | collective-permute-start | bytes 101384 | tf_op jit(solution)/shard_map/ppermute | solution.py:30
  178.3 5.3 %collective-permute-start.20 = (f32[8448]{0:T(1024)S(1)}, f32[8448]{0:T(1024)S(1)}, u32[]{:S(2)}, u32[]{:S(2)}) collective-permute-start(f32[8448]{0:T(1024)S(1)} %reshape.548), channel_id=1, source_target_pairs={{0,8},{8,16},{16,24},{1,9},{9,17},{17,25},{2,10},{10,18},{18,26},{... | collective-permute-start | bytes 101384 | tf_op jit(solution)/shard_map/ppermute | solution.py:28
  184.8 8.7 %collective-permute-start.22 = (f32[924]{0:T(1024)S(1)}, f32[924]{0:T(1024)S(1)}, u32[]{:S(2)}, u32[]{:S(2)}) collective-permute-start(f32[924]{0:T(1024)S(1)} %reshape.552), channel_id=1, source_target_pairs={{0,1},{1,2},{2,3},{3,4},{4,5},{5,6},{6,7},{8,9},{9,10},{10,11},{11... | collective-permute-start | bytes 11096 | tf_op jit(solution)/shard_map/ppermute | solution.py:28
  191.4 7.0 %collective-permute-start.23 = (f32[924]{0:T(1024)S(1)}, f32[924]{0:T(1024)S(1)}, u32[]{:S(2)}, u32[]{:S(2)}) collective-permute-start(f32[924]{0:T(1024)S(1)} %reshape.554), channel_id=1, source_target_pairs={{1,0},{2,1},{3,2},{4,3},{5,4},{6,5},{7,6},{9,8},{10,9},{11,10},{12... | collective-permute-start | bytes 11096 | tf_op jit(solution)/shard_map/ppermute | solution.py:30
  (10 other events, 104.7 us)

commit v2 on v1

--- a/solution.py
+++ b/solution.py
@@ -163,9 +163,9 @@
     exists = exists_x[:, :, None, None] * exists_y[:, None, :, None] * exists_z[:, None, None, :]
     squares = jnp.array([l * l for l in LENGTHS], jnp.float32)
     weight = jnp.sum(exists * squares[:, None, None, None], axis=0)
-    shifts = jnp.arange(8, dtype=jnp.int32)
-    bits = jnp.right_shift(broken[:, None], shifts[None, :, None, None, None]) & 1
-    bits = bits.reshape((broken.shape[0] * 8,) + tuple(cell_shape))[:count]
+    shifts = jnp.array([number % 8 for number in range(count)], jnp.int32)[:, None, None, None]
+    words = jnp.repeat(broken, 8, axis=0)[:count]
+    bits = jnp.right_shift(words, shifts) & 1
     intact = exists * (1.0 - bits.astype(jnp.float32))
     stiffness = 15.0 * shear_modulus / weight
     load_force = loaded.astype(jnp.float32)[None] * blast_load

time: 215 us -> 215 us (level)
  no operation moved by 1% of the time
where the time goes in v2:
time: 215 us; the launch traced here: 213 us
  starting transfers between devices  78.9 us (37%)
  Pallas kernels  63.3 us (29%)
  waiting for transfers between devices  35.9 us (17%)
  other arithmetic  19.3 us (9%)
  local copies, waits for them, and re-layouts  14.4 us (7%)
    ppermute x12, starting transfers between devices, extended_2(): lax.ppermute(tail.reshape(-1), axis, [(i, (i + 1) % count) for i in range...  45.5 us
    pallas_call x2, Pallas kernels, local(): pl.pallas_call(stretch_kernel, out_shape=(jax.ShapeDtypeStruct((count,) +...  35.2 us
    ppermute x12, starting transfers between devices, extended_2(): lax.ppermute(head.reshape(-1), axis, [((i + 1) % count, i) for i in range...  33.4 us
    pallas_call x2, Pallas kernels, local(): pl.pallas_call(force_kernel, out_shape=(jax.ShapeDtypeStruct(displacement...  28.1 us
    ppermute x12, waiting for transfers between devices, extended_2(): lax.ppermute(tail.reshape(-1), axis, [(i, (i + 1) % count) for i in range...  18.5 us
    ppermute x12, waiting for transfers between devices, extended_2(): lax.ppermute(head.reshape(-1), axis, [((i + 1) % count, i) for i in range...  17.4 us
    concatenate x12, other arithmetic, extended_2(): jnp.concatenate([lax.ppermute(tail.reshape(-1), axis, [(i, (i + 1) % coun...  9.5 us
    mul x1, other arithmetic, local(): intact = exists * (1.0 - bits.astype(jnp.float32))  6.23 us
  transfers between devices with their start and end apart: 24, of which 13 were waited for; matrix products, arithmetic and copies ran while one was open for 3% of the time, Pallas kernels for 0%

profile of v2, /device:TPU:106, one launch (start us, length us, event | category | flops | bytes accessed | tf_op | source)
XLA Modules:
  0.0 213.3 jit_solution(14406594318758134829)
XLA Ops:
  4.3 6.2 %multiply_multiply_fusion = (f32[122,16,8,128]{3,2,1,0:T(8,128)}, f32[16,8,128]{2,1,0:T(8,128)S(1)}) fusion(s32[128,16,8,128]{3,2,1,0:T(8,128)S(1)} %bitcast.25, s32[122]{0:T(128)S(1)} %copy-done.9, f32[122,128]{1,0:T(8,128)S(1)} %stack.20, f32[122,16,8]{2,1,0:T(8,128)S(1)} %broadcast_multiply_fusion, f32[122]{0:T(128)S(1)} %copy-done.10), kind=kLoop, calls=%fused_computation | loop fusion | flops 15974400 | bytes 16182224 | tf_op jit(solution)/shard_map/mul | solution.py:169
  13.3 5.0 %collective-permute-start = (f32[12288]{0:T(1024)S(1)}, f32[12288]{0:T(1024)S(1)}, u32[]{:S(2)}, u32[]{:S(2)}) collective-permute-start(f32[12288]{0:T(1024)S(1)} %bitcast.50), channel_id=1, source_target_pairs={{0,32},{32,64},{64,96},{96,128},{128,160},{160,192},{192,224},{1,3... | collective-permute-start | bytes 147464 | tf_op jit(solution)/shard_map/ppermute | solution.py:28
  22.2 2.4 %collective-permute-start.2 = (f32[33792]{0:T(1024)S(1)}, f32[33792]{0:T(1024)S(1)}, u32[]{:S(2)}, u32[]{:S(2)}) collective-permute-start(f32[33792]{0:T(1024)S(1)} %reshape.512), channel_id=1, source_target_pairs={{0,8},{8,16},{16,24},{1,9},{9,17},{17,25},{2,10},{10,18},{18,26},{... | collective-permute-start | bytes 405512 | tf_op jit(solution)/shard_map/ppermute | solution.py:28
  24.7 3.8 %collective-permute-done.2 = f32[33792]{0:T(1024)S(1)} collective-permute-done((f32[33792]{0:T(1024)S(1)}, f32[33792]{0:T(1024)S(1)}, u32[]{:S(2)}, u32[]{:S(2)}) %collective-permute-start.2) | collective-permute-done | bytes 135200 | tf_op jit(solution)/shard_map/ppermute | solution.py:28
  29.3 4.0 %collective-permute-start.4 = (f32[3696]{0:T(1024)S(1)}, f32[3696]{0:T(1024)S(1)}, u32[]{:S(2)}, u32[]{:S(2)}) collective-permute-start(f32[3696]{0:T(1024)S(1)} %reshape.516), channel_id=1, source_target_pairs={{0,1},{1,2},{2,3},{3,4},{4,5},{5,6},{6,7},{8,9},{9,10},{10,11},{11... | collective-permute-start | bytes 44360 | tf_op jit(solution)/shard_map/ppermute | solution.py:28
  33.7 4.2 %collective-permute-start.5 = (f32[3696]{0:T(1024)S(1)}, f32[3696]{0:T(1024)S(1)}, u32[]{:S(2)}, u32[]{:S(2)}) collective-permute-start(f32[3696]{0:T(1024)S(1)} %reshape.518), channel_id=1, source_target_pairs={{1,0},{2,1},{3,2},{4,3},{5,4},{6,5},{7,6},{9,8},{10,9},{11,10},{12... | collective-permute-start | bytes 44360 | tf_op jit(solution)/shard_map/ppermute | solution.py:30
  38.3 2.6 %collective-permute-done.5 = f32[3696]{0:T(1024)S(1)} collective-permute-done((f32[3696]{0:T(1024)S(1)}, f32[3696]{0:T(1024)S(1)}, u32[]{:S(2)}, u32[]{:S(2)}) %collective-permute-start.5) | collective-permute-done | bytes 14816 | tf_op jit(solution)/shard_map/ppermute | solution.py:30
  44.4 17.6 %shard_map.104 = (f32[122,16,8,128]{3,2,1,0:T(8,128)}, f32[16,8,128]{2,1,0:T(8,128)}) custom-call(f32[3,22,14,134]{3,2,1,0:T(8,128)} %slice.112.ext_ref, f32[122,16,8,128]{3,2,1,0:T(8,128)} %get-tuple-element.14.intact_ref, f32[16,8,128]{2,1,0:T(8,128)} %copy-done.3, f32[16,8,128]{2,1,0:T(8,128)} %get-tuple-element.40.factor_ref), custom_call_target="tpu_custom_call" | custom-call | tf_op jit(solution)/shard_map/pallas_call | solution.py:192
  62.7 5.4 %collective-permute-start.6 = (f32[3072]{0:T(1024)S(1)}, f32[3072]{0:T(1024)S(1)}, u32[]{:S(2)}, u32[]{:S(2)}) collective-permute-start(f32[3072]{0:T(1024)S(1)} %get-tuple-element.38), channel_id=1, source_target_pairs={{0,32},{32,64},{64,96},{96,128},{128,160},{160,192},{192,224},{1,3... | collective-permute-start | bytes 36872 | tf_op jit(solution)/shard_map/ppermute | solution.py:28
  71.1 3.8 %collective-permute-done.7 = f32[3072]{0:T(1024)S(1)} collective-permute-done((f32[3072]{0:T(1024)S(1)}, f32[3072]{0:T(1024)S(1)}, u32[]{:S(2)}, u32[]{:S(2)}) %collective-permute-start.7) | collective-permute-done | bytes 12320 | tf_op jit(solution)/shard_map/ppermute | solution.py:30
  84.5 5.1 %collective-permute-start.11 = (f32[924]{0:T(1024)S(1)}, f32[924]{0:T(1024)S(1)}, u32[]{:S(2)}, u32[]{:S(2)}) collective-permute-start(f32[924]{0:T(1024)S(1)} %reshape.531), channel_id=1, source_target_pairs={{1,0},{2,1},{3,2},{4,3},{5,4},{6,5},{7,6},{9,8},{10,9},{11,10},{12... | collective-permute-start | bytes 11096 | tf_op jit(solution)/shard_map/ppermute | solution.py:30
  93.6 3.9 %collective-permute-done.10 = f32[924]{0:T(1024)S(1)} collective-permute-done((f32[924]{0:T(1024)S(1)}, f32[924]{0:T(1024)S(1)}, u32[]{:S(2)}, u32[]{:S(2)}) %collective-permute-start.10) | collective-permute-done | bytes 3728 | tf_op jit(solution)/shard_map/ppermute | solution.py:28
  99.0 14.0 %shard_map.105 = (f32[3,16,8,128]{3,2,1,0:T(8,128)}, f32[3,16,8,128]{3,2,1,0:T(8,128)}) custom-call(f32[22,14,134]{2,1,0:T(8,128)} %pad_maximum_fusion.5.pc_ref, f32[22,14,134]{2,1,0:T(8,128)} %slice_bitcast_fusion.ps_ref, f32[122,16,8,128]{3,2,1,0:T(8,128)} %get-tuple-element.9.stretch_ref, f32[122,16,8,128]{3,2,1,0:T(8,128)} %get-tuple-element.14.intact_ref, ...), custom_call_target="tpu_custom_call" | custom-call | tf_op jit(solution)/shard_map/pallas_call | solution.py:211
  115.8 5.1 %collective-permute-start.12 = (f32[9216]{0:T(1024)S(1)}, f32[9216]{0:T(1024)S(1)}, u32[]{:S(2)}, u32[]{:S(2)}) collective-permute-start(f32[9216]{0:T(1024)S(1)} %bitcast.52), channel_id=1, source_target_pairs={{0,32},{32,64},{64,96},{96,128},{128,160},{160,192},{192,224},{1,3... | collective-permute-start | bytes 110600 | tf_op jit(solution)/shard_map/ppermute | solution.py:28
  125.6 2.4 %collective-permute-start.14 = (f32[25344]{0:T(1024)S(1)}, f32[25344]{0:T(1024)S(1)}, u32[]{:S(2)}, u32[]{:S(2)}) collective-permute-start(f32[25344]{0:T(1024)S(1)} %reshape.537), channel_id=1, source_target_pairs={{0,8},{8,16},{16,24},{1,9},{9,17},{17,25},{2,10},{10,18},{18,26},{... | collective-permute-start | bytes 304136 | tf_op jit(solution)/shard_map/ppermute | solution.py:28
  128.1 3.5 %collective-permute-done.14 = f32[25344]{0:T(1024)S(1)} collective-permute-done((f32[25344]{0:T(1024)S(1)}, f32[25344]{0:T(1024)S(1)}, u32[]{:S(2)}, u32[]{:S(2)}) %collective-permute-start.14) | collective-permute-done | bytes 101408 | tf_op jit(solution)/shard_map/ppermute | solution.py:28
  134.6 6.3 %collective-permute-start.17 = (f32[2772]{0:T(1024)S(1)}, f32[2772]{0:T(1024)S(1)}, u32[]{:S(2)}, u32[]{:S(2)}) collective-permute-start(f32[2772]{0:T(1024)S(1)} %reshape.543), channel_id=1, source_target_pairs={{1,0},{2,1},{3,2},{4,3},{5,4},{6,5},{7,6},{9,8},{10,9},{11,10},{12... | collective-permute-start | bytes 33272 | tf_op jit(solution)/shard_map/ppermute | solution.py:30
  144.4 17.6 %shard_map.106 = (f32[122,16,8,128]{3,2,1,0:T(8,128)}, f32[16,8,128]{2,1,0:T(8,128)}) custom-call(f32[3,22,14,134]{3,2,1,0:T(8,128)} %pad_maximum_fusion.1.ext_ref, f32[122,16,8,128]{3,2,1,0:T(8,128)} %get-tuple-element.14.intact_ref, f32[16,8,128]{2,1,0:T(8,128)} %copy-done.3, f32[16,8,128]{2,1,0:T(8,128)} %get-tuple-element.40.factor_ref), custom_call_target="tpu_custom_call" | custom-call | tf_op jit(solution)/shard_map/pallas_call | solution.py:192
  162.8 5.5 %collective-permute-start.18 = (f32[3072]{0:T(1024)S(1)}, f32[3072]{0:T(1024)S(1)}, u32[]{:S(2)}, u32[]{:S(2)}) collective-permute-start(f32[3072]{0:T(1024)S(1)} %get-tuple-element.36), channel_id=1, source_target_pairs={{0,32},{32,64},{64,96},{96,128},{128,160},{160,192},{192,224},{1,3... | collective-permute-start | bytes 36872 | tf_op jit(solution)/shard_map/ppermute | solution.py:28
  170.2 4.9 %collective-permute-done.19 = f32[3072]{0:T(1024)S(1)} collective-permute-done((f32[3072]{0:T(1024)S(1)}, f32[3072]{0:T(1024)S(1)}, u32[]{:S(2)}, u32[]{:S(2)}) %collective-permute-start.19) | collective-permute-done | bytes 12320 | tf_op jit(solution)/shard_map/ppermute | solution.py:30
  180.4 2.8 %collective-permute-done.20 = f32[8448]{0:T(1024)S(1)} collective-permute-done((f32[8448]{0:T(1024)S(1)}, f32[8448]{0:T(1024)S(1)}, u32[]{:S(2)}, u32[]{:S(2)}) %collective-permute-start.20) | collective-permute-done | bytes 33824 | tf_op jit(solution)/shard_map/ppermute | solution.py:28
  184.4 6.3 %collective-permute-start.22 = (f32[924]{0:T(1024)S(1)}, f32[924]{0:T(1024)S(1)}, u32[]{:S(2)}, u32[]{:S(2)}) collective-permute-start(f32[924]{0:T(1024)S(1)} %reshape.553), channel_id=1, source_target_pairs={{0,1},{1,2},{2,3},{3,4},{4,5},{5,6},{6,7},{8,9},{9,10},{10,11},{11... | collective-permute-start | bytes 11096 | tf_op jit(solution)/shard_map/ppermute | solution.py:28
  193.4 4.6 %collective-permute-done.23 = f32[924]{0:T(1024)S(1)} collective-permute-done((f32[924]{0:T(1024)S(1)}, f32[924]{0:T(1024)S(1)}, u32[]{:S(2)}, u32[]{:S(2)}) %collective-permute-start.23) | collective-permute-done | bytes 3728 | tf_op jit(solution)/shard_map/ppermute | solution.py:30
  199.2 14.0 %shard_map.107 = (f32[3,16,8,128]{3,2,1,0:T(8,128)}, f32[3,16,8,128]{3,2,1,0:T(8,128)}) custom-call(f32[22,14,134]{2,1,0:T(8,128)} %pad_maximum_fusion.6.pc_ref, f32[22,14,134]{2,1,0:T(8,128)} %slice_bitcast_fusion.ps_ref, f32[122,16,8,128]{3,2,1,0:T(8,128)} %get-tuple-element.12.stretch_ref, f32[122,16,8,128]{3,2,1,0:T(8,128)} %get-tuple-element.14.intact_ref, ...), custom_call_target="tpu_custom_call" | custom-call | tf_op jit(solution)/shard_map/pallas_call | solution.py:211
  (141 shorter events, 60.5 us)
Async XLA Ops:
  11.2 7.2 %collective-permute-start.1 = (f32[12288]{0:T(1024)S(1)}, f32[12288]{0:T(1024)S(1)}, u32[]{:S(2)}, u32[]{:S(2)}) collective-permute-start(f32[12288]{0:T(1024)S(1)} %bitcast.51), channel_id=1, source_target_pairs={{32,0},{64,32},{96,64},{128,96},{160,128},{192,160},{224,192},{33,... | collective-permute-start | bytes 147464 | tf_op jit(solution)/shard_map/ppermute | solution.py:30
  13.3 6.8 %collective-permute-start = (f32[12288]{0:T(1024)S(1)}, f32[12288]{0:T(1024)S(1)}, u32[]{:S(2)}, u32[]{:S(2)}) collective-permute-start(f32[12288]{0:T(1024)S(1)} %bitcast.50), channel_id=1, source_target_pairs={{0,32},{32,64},{64,96},{96,128},{128,160},{160,192},{192,224},{1,3... | collective-permute-start | bytes 147464 | tf_op jit(solution)/shard_map/ppermute | solution.py:28
  20.2 4.5 %collective-permute-start.3 = (f32[33792]{0:T(1024)S(1)}, f32[33792]{0:T(1024)S(1)}, u32[]{:S(2)}, u32[]{:S(2)}) collective-permute-start(f32[33792]{0:T(1024)S(1)} %reshape.514), channel_id=1, source_target_pairs={{8,0},{16,8},{24,16},{9,1},{17,9},{25,17},{10,2},{18,10},{26,18},{... | collective-permute-start | bytes 405512 | tf_op jit(solution)/shard_map/ppermute | solution.py:30
  22.2 6.3 %collective-permute-start.2 = (f32[33792]{0:T(1024)S(1)}, f32[33792]{0:T(1024)S(1)}, u32[]{:S(2)}, u32[]{:S(2)}) collective-permute-start(f32[33792]{0:T(1024)S(1)} %reshape.512), channel_id=1, source_target_pairs={{0,8},{8,16},{16,24},{1,9},{9,17},{17,25},{2,10},{10,18},{18,26},{... | collective-permute-start | bytes 405512 | tf_op jit(solution)/shard_map/ppermute | solution.py:28
  29.3 8.6 %collective-permute-start.4 = (f32[3696]{0:T(1024)S(1)}, f32[3696]{0:T(1024)S(1)}, u32[]{:S(2)}, u32[]{:S(2)}) collective-permute-start(f32[3696]{0:T(1024)S(1)} %reshape.516), channel_id=1, source_target_pairs={{0,1},{1,2},{2,3},{3,4},{4,5},{5,6},{6,7},{8,9},{9,10},{10,11},{11... | collective-permute-start | bytes 44360 | tf_op jit(solution)/shard_map/ppermute | solution.py:28
  33.7 7.1 %collective-permute-start.5 = (f32[3696]{0:T(1024)S(1)}, f32[3696]{0:T(1024)S(1)}, u32[]{:S(2)}, u32[]{:S(2)}) collective-permute-start(f32[3696]{0:T(1024)S(1)} %reshape.518), channel_id=1, source_target_pairs={{1,0},{2,1},{3,2},{4,3},{5,4},{6,5},{7,6},{9,8},{10,9},{11,10},{12... | collective-permute-start | bytes 44360 | tf_op jit(solution)/shard_map/ppermute | solution.py:30
  62.7 8.4 %collective-permute-start.6 = (f32[3072]{0:T(1024)S(1)}, f32[3072]{0:T(1024)S(1)}, u32[]{:S(2)}, u32[]{:S(2)}) collective-permute-start(f32[3072]{0:T(1024)S(1)} %get-tuple-element.38), channel_id=1, source_target_pairs={{0,32},{32,64},{64,96},{96,128},{128,160},{160,192},{192,224},{1,3... | collective-permute-start | bytes 36872 | tf_op jit(solution)/shard_map/ppermute | solution.py:28
  68.2 6.8 %collective-permute-start.7 = (f32[3072]{0:T(1024)S(1)}, f32[3072]{0:T(1024)S(1)}, u32[]{:S(2)}, u32[]{:S(2)}) collective-permute-start(f32[3072]{0:T(1024)S(1)} %get-tuple-element.39), channel_id=1, source_target_pairs={{32,0},{64,32},{96,64},{128,96},{160,128},{192,160},{224,192},{33,... | collective-permute-start | bytes 36872 | tf_op jit(solution)/shard_map/ppermute | solution.py:30
  75.9 6.0 %collective-permute-start.9 = (f32[8448]{0:T(1024)S(1)}, f32[8448]{0:T(1024)S(1)}, u32[]{:S(2)}, u32[]{:S(2)}) collective-permute-start(f32[8448]{0:T(1024)S(1)} %reshape.527), channel_id=1, source_target_pairs={{8,0},{16,8},{24,16},{9,1},{17,9},{25,17},{10,2},{18,10},{26,18},{... | collective-permute-start | bytes 101384 | tf_op jit(solution)/shard_map/ppermute | solution.py:30
  77.8 5.3 %collective-permute-start.8 = (f32[8448]{0:T(1024)S(1)}, f32[8448]{0:T(1024)S(1)}, u32[]{:S(2)}, u32[]{:S(2)}) collective-permute-start(f32[8448]{0:T(1024)S(1)} %reshape.525), channel_id=1, source_target_pairs={{0,8},{8,16},{16,24},{1,9},{9,17},{17,25},{2,10},{10,18},{18,26},{... | collective-permute-start | bytes 101384 | tf_op jit(solution)/shard_map/ppermute | solution.py:28
  84.5 13.2 %collective-permute-start.11 = (f32[924]{0:T(1024)S(1)}, f32[924]{0:T(1024)S(1)}, u32[]{:S(2)}, u32[]{:S(2)}) collective-permute-start(f32[924]{0:T(1024)S(1)} %reshape.531), channel_id=1, source_target_pairs={{1,0},{2,1},{3,2},{4,3},{5,4},{6,5},{7,6},{9,8},{10,9},{11,10},{12... | collective-permute-start | bytes 11096 | tf_op jit(solution)/shard_map/ppermute | solution.py:30
  89.6 7.9 %collective-permute-start.10 = (f32[924]{0:T(1024)S(1)}, f32[924]{0:T(1024)S(1)}, u32[]{:S(2)}, u32[]{:S(2)}) collective-permute-start(f32[924]{0:T(1024)S(1)} %reshape.529), channel_id=1, source_target_pairs={{0,1},{1,2},{2,3},{3,4},{4,5},{5,6},{6,7},{8,9},{9,10},{10,11},{11... | collective-permute-start | bytes 11096 | tf_op jit(solution)/shard_map/ppermute | solution.py:28
  113.9 7.1 %collective-permute-start.13 = (f32[9216]{0:T(1024)S(1)}, f32[9216]{0:T(1024)S(1)}, u32[]{:S(2)}, u32[]{:S(2)}) collective-permute-start(f32[9216]{0:T(1024)S(1)} %bitcast.53), channel_id=1, source_target_pairs={{32,0},{64,32},{96,64},{128,96},{160,128},{192,160},{224,192},{33,... | collective-permute-start | bytes 110600 | tf_op jit(solution)/shard_map/ppermute | solution.py:30
  115.8 6.8 %collective-permute-start.12 = (f32[9216]{0:T(1024)S(1)}, f32[9216]{0:T(1024)S(1)}, u32[]{:S(2)}, u32[]{:S(2)}) collective-permute-start(f32[9216]{0:T(1024)S(1)} %bitcast.52), channel_id=1, source_target_pairs={{0,32},{32,64},{64,96},{96,128},{128,160},{160,192},{192,224},{1,3... | collective-permute-start | bytes 110600 | tf_op jit(solution)/shard_map/ppermute | solution.py:28
  123.6 4.4 %collective-permute-start.15 = (f32[25344]{0:T(1024)S(1)}, f32[25344]{0:T(1024)S(1)}, u32[]{:S(2)}, u32[]{:S(2)}) collective-permute-start(f32[25344]{0:T(1024)S(1)} %reshape.539), channel_id=1, source_target_pairs={{8,0},{16,8},{24,16},{9,1},{17,9},{25,17},{10,2},{18,10},{26,18},{... | collective-permute-start | bytes 304136 | tf_op jit(solution)/shard_map/ppermute | solution.py:30
  125.6 6.0 %collective-permute-start.14 = (f32[25344]{0:T(1024)S(1)}, f32[25344]{0:T(1024)S(1)}, u32[]{:S(2)}, u32[]{:S(2)}) collective-permute-start(f32[25344]{0:T(1024)S(1)} %reshape.537), channel_id=1, source_target_pairs={{0,8},{8,16},{16,24},{1,9},{9,17},{17,25},{2,10},{10,18},{18,26},{... | collective-permute-start | bytes 304136 | tf_op jit(solution)/shard_map/ppermute | solution.py:28
  132.1 8.7 %collective-permute-start.16 = (f32[2772]{0:T(1024)S(1)}, f32[2772]{0:T(1024)S(1)}, u32[]{:S(2)}, u32[]{:S(2)}) collective-permute-start(f32[2772]{0:T(1024)S(1)} %reshape.541), channel_id=1, source_target_pairs={{0,1},{1,2},{2,3},{3,4},{4,5},{5,6},{6,7},{8,9},{9,10},{10,11},{11... | collective-permute-start | bytes 33272 | tf_op jit(solution)/shard_map/ppermute | solution.py:28
  134.6 7.8 %collective-permute-start.17 = (f32[2772]{0:T(1024)S(1)}, f32[2772]{0:T(1024)S(1)}, u32[]{:S(2)}, u32[]{:S(2)}) collective-permute-start(f32[2772]{0:T(1024)S(1)} %reshape.543), channel_id=1, source_target_pairs={{1,0},{2,1},{3,2},{4,3},{5,4},{6,5},{7,6},{9,8},{10,9},{11,10},{12... | collective-permute-start | bytes 33272 | tf_op jit(solution)/shard_map/ppermute | solution.py:30
  162.8 7.4 %collective-permute-start.18 = (f32[3072]{0:T(1024)S(1)}, f32[3072]{0:T(1024)S(1)}, u32[]{:S(2)}, u32[]{:S(2)}) collective-permute-start(f32[3072]{0:T(1024)S(1)} %get-tuple-element.36), channel_id=1, source_target_pairs={{0,32},{32,64},{64,96},{96,128},{128,160},{160,192},{192,224},{1,3... | collective-permute-start | bytes 36872 | tf_op jit(solution)/shard_map/ppermute | solution.py:28
  168.3 6.8 %collective-permute-start.19 = (f32[3072]{0:T(1024)S(1)}, f32[3072]{0:T(1024)S(1)}, u32[]{:S(2)}, u32[]{:S(2)}) collective-permute-start(f32[3072]{0:T(1024)S(1)} %get-tuple-element.37), channel_id=1, source_target_pairs={{32,0},{64,32},{96,64},{128,96},{160,128},{192,160},{224,192},{33,... | collective-permute-start | bytes 36872 | tf_op jit(solution)/shard_map/ppermute | solution.py:30
  176.0 4.4 %collective-permute-start.21 = (f32[8448]{0:T(1024)S(1)}, f32[8448]{0:T(1024)S(1)}, u32[]{:S(2)}, u32[]{:S(2)}) collective-permute-start(f32[8448]{0:T(1024)S(1)} %reshape.551), channel_id=1, source_target_pairs={{8,0},{16,8},{24,16},{9,1},{17,9},{25,17},{10,2},{18,10},{26,18},{... | collective-permute-start | bytes 101384 | tf_op jit(solution)/shard_map/ppermute | solution.py:30
  177.9 5.3 %collective-permute-start.20 = (f32[8448]{0:T(1024)S(1)}, f32[8448]{0:T(1024)S(1)}, u32[]{:S(2)}, u32[]{:S(2)}) collective-permute-start(f32[8448]{0:T(1024)S(1)} %reshape.549), channel_id=1, source_target_pairs={{0,8},{8,16},{16,24},{1,9},{9,17},{17,25},{2,10},{10,18},{18,26},{... | collective-permute-start | bytes 101384 | tf_op jit(solution)/shard_map/ppermute | solution.py:28
  184.4 8.7 %collective-permute-start.22 = (f32[924]{0:T(1024)S(1)}, f32[924]{0:T(1024)S(1)}, u32[]{:S(2)}, u32[]{:S(2)}) collective-permute-start(f32[924]{0:T(1024)S(1)} %reshape.553), channel_id=1, source_target_pairs={{0,1},{1,2},{2,3},{3,4},{4,5},{5,6},{6,7},{8,9},{9,10},{10,11},{11... | collective-permute-start | bytes 11096 | tf_op jit(solution)/shard_map/ppermute | solution.py:28
  191.0 7.0 %collective-permute-start.23 = (f32[924]{0:T(1024)S(1)}, f32[924]{0:T(1024)S(1)}, u32[]{:S(2)}, u32[]{:S(2)}) collective-permute-start(f32[924]{0:T(1024)S(1)} %reshape.555), channel_id=1, source_target_pairs={{1,0},{2,1},{3,2},{4,3},{5,4},{6,5},{7,6},{9,8},{10,9},{11,10},{12... | collective-permute-start | bytes 11096 | tf_op jit(solution)/shard_map/ppermute | solution.py:30
  (11 other events, 105.7 us)

commit v3 on v2

--- a/solution.py
+++ b/solution.py
@@ -66,17 +66,23 @@
     return extended_2(values, (("gx", 1), ("gy", 2), ("gz", 3)), 3)
 
 
+REACH = {pair: max(abs(e[0]) for e in OFFSETS if (e[1], e[2]) == pair) for pair in PAIRS if pair != (0, 0)}
+REACH[(0, 0)] = 3
+
+
 def fill_stack(stack_ref, padded_ref, leading):
     cells_y, cells_z = stack_ref.shape[-2], stack_ref.shape[-1]
     trips = 2
     chunk = stack_ref.shape[-3] // trips
 
     def rows(trip, carry):
-        start = trip * chunk
         for pair, (oy, oz) in enumerate(PAIRS):
+            skip = 3 - REACH[(oy, oz)]
+            start = trip * chunk + skip * (1 - trip)
+            count = chunk - skip
             for c in leading:
-                target = (pair, pl.ds(start, chunk)) if c is None else (pair, c, pl.ds(start, chunk))
-                source = (pl.ds(start, chunk),) if c is None else (c, pl.ds(start, chunk))
+                target = (pair, pl.ds(start, count)) if c is None else (pair, c, pl.ds(start, count))
+                source = (pl.ds(start, count),) if c is None else (c, pl.ds(start, count))
                 stack_ref[target] = padded_ref[source + (pl.ds(3 + oy, cells_y), pl.ds(3 + oz, cells_z))]
         return carry
 

time: 215 us -> 212 us (0.986)
  Pallas kernels: 63.3 us -> 60.3 us
where the time goes in v3:
time: 212 us; the launch traced here: 210 us
  starting transfers between devices  78.4 us (37%)
  Pallas kernels  60.3 us (28%)
  waiting for transfers between devices  36.4 us (17%)
  other arithmetic  19.3 us (9%)
  local copies, waits for them, and re-layouts  14.4 us (7%)
    ppermute x12, starting transfers between devices, extended_2(): lax.ppermute(tail.reshape(-1), axis, [(i, (i + 1) % count) for i in range...  45.7 us
    pallas_call x2, Pallas kernels, local(): pl.pallas_call(stretch_kernel, out_shape=(jax.ShapeDtypeStruct((count,) +...  33.5 us
    ppermute x12, starting transfers between devices, extended_2(): lax.ppermute(head.reshape(-1), axis, [((i + 1) % count, i) for i in range...  32.7 us
    pallas_call x2, Pallas kernels, local(): pl.pallas_call(force_kernel, out_shape=(jax.ShapeDtypeStruct(displacement...  26.9 us
    ppermute x12, waiting for transfers between devices, extended_2(): lax.ppermute(tail.reshape(-1), axis, [(i, (i + 1) % count) for i in range...  18.3 us
    ppermute x12, waiting for transfers between devices, extended_2(): lax.ppermute(head.reshape(-1), axis, [((i + 1) % count, i) for i in range...  18 us
    concatenate x12, other arithmetic, extended_2(): jnp.concatenate([lax.ppermute(tail.reshape(-1), axis, [(i, (i + 1) % coun...  9.5 us
    mul x1, other arithmetic, local(): intact = exists * (1.0 - bits.astype(jnp.float32))  6.23 us
  transfers between devices with their start and end apart: 24, of which 13 were waited for; matrix products, arithmetic and copies ran while one was open for 3% of the time, Pallas kernels for 0%

profile of v3, /device:TPU:106, one launch (start us, length us, event | category | flops | bytes accessed | tf_op | source)
XLA Modules:
  0.0 210.2 jit_solution(11636684331309956319)
XLA Ops:
  4.3 6.2 %multiply_multiply_fusion = (f32[122,16,8,128]{3,2,1,0:T(8,128)}, f32[16,8,128]{2,1,0:T(8,128)S(1)}) fusion(s32[128,16,8,128]{3,2,1,0:T(8,128)S(1)} %bitcast.25, s32[122]{0:T(128)S(1)} %copy-done.9, f32[122,128]{1,0:T(8,128)S(1)} %stack.20, f32[122,16,8]{2,1,0:T(8,128)S(1)} %broadcast_multiply_fusion, f32[122]{0:T(128)S(1)} %copy-done.10), kind=kLoop, calls=%fused_computation | loop fusion | flops 15974400 | bytes 16182224 | tf_op jit(solution)/shard_map/mul | solution.py:175
  13.3 5.0 %collective-permute-start = (f32[12288]{0:T(1024)S(1)}, f32[12288]{0:T(1024)S(1)}, u32[]{:S(2)}, u32[]{:S(2)}) collective-permute-start(f32[12288]{0:T(1024)S(1)} %bitcast.50), channel_id=1, source_target_pairs={{0,32},{32,64},{64,96},{96,128},{128,160},{160,192},{192,224},{1,3... | collective-permute-start | bytes 147464 | tf_op jit(solution)/shard_map/ppermute | solution.py:28
  22.2 2.4 %collective-permute-start.2 = (f32[33792]{0:T(1024)S(1)}, f32[33792]{0:T(1024)S(1)}, u32[]{:S(2)}, u32[]{:S(2)}) collective-permute-start(f32[33792]{0:T(1024)S(1)} %reshape.512), channel_id=1, source_target_pairs={{0,8},{8,16},{16,24},{1,9},{9,17},{17,25},{2,10},{10,18},{18,26},{... | collective-permute-start | bytes 405512 | tf_op jit(solution)/shard_map/ppermute | solution.py:28
  24.7 3.8 %collective-permute-done.2 = f32[33792]{0:T(1024)S(1)} collective-permute-done((f32[33792]{0:T(1024)S(1)}, f32[33792]{0:T(1024)S(1)}, u32[]{:S(2)}, u32[]{:S(2)}) %collective-permute-start.2) | collective-permute-done | bytes 135200 | tf_op jit(solution)/shard_map/ppermute | solution.py:28
  29.3 4.0 %collective-permute-start.4 = (f32[3696]{0:T(1024)S(1)}, f32[3696]{0:T(1024)S(1)}, u32[]{:S(2)}, u32[]{:S(2)}) collective-permute-start(f32[3696]{0:T(1024)S(1)} %reshape.516), channel_id=1, source_target_pairs={{0,1},{1,2},{2,3},{3,4},{4,5},{5,6},{6,7},{8,9},{9,10},{10,11},{11... | collective-permute-start | bytes 44360 | tf_op jit(solution)/shard_map/ppermute | solution.py:28
  33.7 4.2 %collective-permute-start.5 = (f32[3696]{0:T(1024)S(1)}, f32[3696]{0:T(1024)S(1)}, u32[]{:S(2)}, u32[]{:S(2)}) collective-permute-start(f32[3696]{0:T(1024)S(1)} %reshape.518), channel_id=1, source_target_pairs={{1,0},{2,1},{3,2},{4,3},{5,4},{6,5},{7,6},{9,8},{10,9},{11,10},{12... | collective-permute-start | bytes 44360 | tf_op jit(solution)/shard_map/ppermute | solution.py:30
  38.3 2.6 %collective-permute-done.5 = f32[3696]{0:T(1024)S(1)} collective-permute-done((f32[3696]{0:T(1024)S(1)}, f32[3696]{0:T(1024)S(1)}, u32[]{:S(2)}, u32[]{:S(2)}) %collective-permute-start.5) | collective-permute-done | bytes 14816 | tf_op jit(solution)/shard_map/ppermute | solution.py:30
  44.4 16.7 %shard_map.104 = (f32[122,16,8,128]{3,2,1,0:T(8,128)}, f32[16,8,128]{2,1,0:T(8,128)}) custom-call(f32[3,22,14,134]{3,2,1,0:T(8,128)} %slice.112.ext_ref, f32[122,16,8,128]{3,2,1,0:T(8,128)} %get-tuple-element.14.intact_ref, f32[16,8,128]{2,1,0:T(8,128)} %copy-done.3, f32[16,8,128]{2,1,0:T(8,128)} %get-tuple-element.40.factor_ref), custom_call_target="tpu_custom_call" | custom-call | tf_op jit(solution)/shard_map/pallas_call | solution.py:198
  61.8 5.4 %collective-permute-start.6 = (f32[3072]{0:T(1024)S(1)}, f32[3072]{0:T(1024)S(1)}, u32[]{:S(2)}, u32[]{:S(2)}) collective-permute-start(f32[3072]{0:T(1024)S(1)} %get-tuple-element.38), channel_id=1, source_target_pairs={{0,32},{32,64},{64,96},{96,128},{128,160},{160,192},{192,224},{1,3... | collective-permute-start | bytes 36872 | tf_op jit(solution)/shard_map/ppermute | solution.py:28
  70.0 4.0 %collective-permute-done.7 = f32[3072]{0:T(1024)S(1)} collective-permute-done((f32[3072]{0:T(1024)S(1)}, f32[3072]{0:T(1024)S(1)}, u32[]{:S(2)}, u32[]{:S(2)}) %collective-permute-start.7) | collective-permute-done | bytes 12320 | tf_op jit(solution)/shard_map/ppermute | solution.py:30
  76.9 2.6 %collective-permute-start.8 = (f32[8448]{0:T(1024)S(1)}, f32[8448]{0:T(1024)S(1)}, u32[]{:S(2)}, u32[]{:S(2)}) collective-permute-start(f32[8448]{0:T(1024)S(1)} %reshape.525), channel_id=1, source_target_pairs={{0,8},{8,16},{16,24},{1,9},{9,17},{17,25},{2,10},{10,18},{18,26},{... | collective-permute-start | bytes 101384 | tf_op jit(solution)/shard_map/ppermute | solution.py:28
  83.6 5.1 %collective-permute-start.11 = (f32[924]{0:T(1024)S(1)}, f32[924]{0:T(1024)S(1)}, u32[]{:S(2)}, u32[]{:S(2)}) collective-permute-start(f32[924]{0:T(1024)S(1)} %reshape.531), channel_id=1, source_target_pairs={{1,0},{2,1},{3,2},{4,3},{5,4},{6,5},{7,6},{9,8},{10,9},{11,10},{12... | collective-permute-start | bytes 11096 | tf_op jit(solution)/shard_map/ppermute | solution.py:30
  92.7 3.9 %collective-permute-done.10 = f32[924]{0:T(1024)S(1)} collective-permute-done((f32[924]{0:T(1024)S(1)}, f32[924]{0:T(1024)S(1)}, u32[]{:S(2)}, u32[]{:S(2)}) %collective-permute-start.10) | collective-permute-done | bytes 3728 | tf_op jit(solution)/shard_map/ppermute | solution.py:28
  98.1 13.4 %shard_map.105 = (f32[3,16,8,128]{3,2,1,0:T(8,128)}, f32[3,16,8,128]{3,2,1,0:T(8,128)}) custom-call(f32[22,14,134]{2,1,0:T(8,128)} %pad_maximum_fusion.5.pc_ref, f32[22,14,134]{2,1,0:T(8,128)} %slice_bitcast_fusion.ps_ref, f32[122,16,8,128]{3,2,1,0:T(8,128)} %get-tuple-element.9.stretch_ref, f32[122,16,8,128]{3,2,1,0:T(8,128)} %get-tuple-element.14.intact_ref, ...), custom_call_target="tpu_custom_call" | custom-call | tf_op jit(solution)/shard_map/pallas_call | solution.py:217
  114.3 5.1 %collective-permute-start.12 = (f32[9216]{0:T(1024)S(1)}, f32[9216]{0:T(1024)S(1)}, u32[]{:S(2)}, u32[]{:S(2)}) collective-permute-start(f32[9216]{0:T(1024)S(1)} %bitcast.52), channel_id=1, source_target_pairs={{0,32},{32,64},{64,96},{96,128},{128,160},{160,192},{192,224},{1,3... | collective-permute-start | bytes 110600 | tf_op jit(solution)/shard_map/ppermute | solution.py:28
  126.6 3.5 %collective-permute-done.14 = f32[25344]{0:T(1024)S(1)} collective-permute-done((f32[25344]{0:T(1024)S(1)}, f32[25344]{0:T(1024)S(1)}, u32[]{:S(2)}, u32[]{:S(2)}) %collective-permute-start.14) | collective-permute-done | bytes 101408 | tf_op jit(solution)/shard_map/ppermute | solution.py:28
  133.1 6.0 %collective-permute-start.17 = (f32[2772]{0:T(1024)S(1)}, f32[2772]{0:T(1024)S(1)}, u32[]{:S(2)}, u32[]{:S(2)}) collective-permute-start(f32[2772]{0:T(1024)S(1)} %reshape.543), channel_id=1, source_target_pairs={{1,0},{2,1},{3,2},{4,3},{5,4},{6,5},{7,6},{9,8},{10,9},{11,10},{12... | collective-permute-start | bytes 33272 | tf_op jit(solution)/shard_map/ppermute | solution.py:30
  142.9 16.7 %shard_map.106 = (f32[122,16,8,128]{3,2,1,0:T(8,128)}, f32[16,8,128]{2,1,0:T(8,128)}) custom-call(f32[3,22,14,134]{3,2,1,0:T(8,128)} %pad_maximum_fusion.1.ext_ref, f32[122,16,8,128]{3,2,1,0:T(8,128)} %get-tuple-element.14.intact_ref, f32[16,8,128]{2,1,0:T(8,128)} %copy-done.3, f32[16,8,128]{2,1,0:T(8,128)} %get-tuple-element.40.factor_ref), custom_call_target="tpu_custom_call" | custom-call | tf_op jit(solution)/shard_map/pallas_call | solution.py:198
  160.4 5.4 %collective-permute-start.18 = (f32[3072]{0:T(1024)S(1)}, f32[3072]{0:T(1024)S(1)}, u32[]{:S(2)}, u32[]{:S(2)}) collective-permute-start(f32[3072]{0:T(1024)S(1)} %get-tuple-element.36), channel_id=1, source_target_pairs={{0,32},{32,64},{64,96},{96,128},{128,160},{160,192},{192,224},{1,3... | collective-permute-start | bytes 36872 | tf_op jit(solution)/shard_map/ppermute | solution.py:28
  167.8 4.9 %collective-permute-done.19 = f32[3072]{0:T(1024)S(1)} collective-permute-done((f32[3072]{0:T(1024)S(1)}, f32[3072]{0:T(1024)S(1)}, u32[]{:S(2)}, u32[]{:S(2)}) %collective-permute-start.19) | collective-permute-done | bytes 12320 | tf_op jit(solution)/shard_map/ppermute | solution.py:30
  177.9 2.8 %collective-permute-done.20 = f32[8448]{0:T(1024)S(1)} collective-permute-done((f32[8448]{0:T(1024)S(1)}, f32[8448]{0:T(1024)S(1)}, u32[]{:S(2)}, u32[]{:S(2)}) %collective-permute-start.20) | collective-permute-done | bytes 33824 | tf_op jit(solution)/shard_map/ppermute | solution.py:28
  182.0 6.3 %collective-permute-start.22 = (f32[924]{0:T(1024)S(1)}, f32[924]{0:T(1024)S(1)}, u32[]{:S(2)}, u32[]{:S(2)}) collective-permute-start(f32[924]{0:T(1024)S(1)} %reshape.553), channel_id=1, source_target_pairs={{0,1},{1,2},{2,3},{3,4},{4,5},{5,6},{6,7},{8,9},{9,10},{10,11},{11... | collective-permute-start | bytes 11096 | tf_op jit(solution)/shard_map/ppermute | solution.py:28
  190.7 4.9 %collective-permute-done.23 = f32[924]{0:T(1024)S(1)} collective-permute-done((f32[924]{0:T(1024)S(1)}, f32[924]{0:T(1024)S(1)}, u32[]{:S(2)}, u32[]{:S(2)}) %collective-permute-start.23) | collective-permute-done | bytes 3728 | tf_op jit(solution)/shard_map/ppermute | solution.py:30
  196.8 13.4 %shard_map.107 = (f32[3,16,8,128]{3,2,1,0:T(8,128)}, f32[3,16,8,128]{3,2,1,0:T(8,128)}) custom-call(f32[22,14,134]{2,1,0:T(8,128)} %pad_maximum_fusion.6.pc_ref, f32[22,14,134]{2,1,0:T(8,128)} %slice_bitcast_fusion.ps_ref, f32[122,16,8,128]{3,2,1,0:T(8,128)} %get-tuple-element.12.stretch_ref, f32[122,16,8,128]{3,2,1,0:T(8,128)} %get-tuple-element.14.intact_ref, ...), custom_call_target="tpu_custom_call" | custom-call | tf_op jit(solution)/shard_map/pallas_call | solution.py:217
  (141 shorter events, 60.2 us)
Async XLA Ops:
  11.2 7.2 %collective-permute-start.1 = (f32[12288]{0:T(1024)S(1)}, f32[12288]{0:T(1024)S(1)}, u32[]{:S(2)}, u32[]{:S(2)}) collective-permute-start(f32[12288]{0:T(1024)S(1)} %bitcast.51), channel_id=1, source_target_pairs={{32,0},{64,32},{96,64},{128,96},{160,128},{192,160},{224,192},{33,... | collective-permute-start | bytes 147464 | tf_op jit(solution)/shard_map/ppermute | solution.py:30
  13.3 6.8 %collective-permute-start = (f32[12288]{0:T(1024)S(1)}, f32[12288]{0:T(1024)S(1)}, u32[]{:S(2)}, u32[]{:S(2)}) collective-permute-start(f32[12288]{0:T(1024)S(1)} %bitcast.50), channel_id=1, source_target_pairs={{0,32},{32,64},{64,96},{96,128},{128,160},{160,192},{192,224},{1,3... | collective-permute-start | bytes 147464 | tf_op jit(solution)/shard_map/ppermute | solution.py:28
  20.2 4.5 %collective-permute-start.3 = (f32[33792]{0:T(1024)S(1)}, f32[33792]{0:T(1024)S(1)}, u32[]{:S(2)}, u32[]{:S(2)}) collective-permute-start(f32[33792]{0:T(1024)S(1)} %reshape.514), channel_id=1, source_target_pairs={{8,0},{16,8},{24,16},{9,1},{17,9},{25,17},{10,2},{18,10},{26,18},{... | collective-permute-start | bytes 405512 | tf_op jit(solution)/shard_map/ppermute | solution.py:30
  22.2 6.3 %collective-permute-start.2 = (f32[33792]{0:T(1024)S(1)}, f32[33792]{0:T(1024)S(1)}, u32[]{:S(2)}, u32[]{:S(2)}) collective-permute-start(f32[33792]{0:T(1024)S(1)} %reshape.512), channel_id=1, source_target_pairs={{0,8},{8,16},{16,24},{1,9},{9,17},{17,25},{2,10},{10,18},{18,26},{... | collective-permute-start | bytes 405512 | tf_op jit(solution)/shard_map/ppermute | solution.py:28
  29.3 8.6 %collective-permute-start.4 = (f32[3696]{0:T(1024)S(1)}, f32[3696]{0:T(1024)S(1)}, u32[]{:S(2)}, u32[]{:S(2)}) collective-permute-start(f32[3696]{0:T(1024)S(1)} %reshape.516), channel_id=1, source_target_pairs={{0,1},{1,2},{2,3},{3,4},{4,5},{5,6},{6,7},{8,9},{9,10},{10,11},{11... | collective-permute-start | bytes 44360 | tf_op jit(solution)/shard_map/ppermute | solution.py:28
  33.7 7.1 %collective-permute-start.5 = (f32[3696]{0:T(1024)S(1)}, f32[3696]{0:T(1024)S(1)}, u32[]{:S(2)}, u32[]{:S(2)}) collective-permute-start(f32[3696]{0:T(1024)S(1)} %reshape.518), channel_id=1, source_target_pairs={{1,0},{2,1},{3,2},{4,3},{5,4},{6,5},{7,6},{9,8},{10,9},{11,10},{12... | collective-permute-start | bytes 44360 | tf_op jit(solution)/shard_map/ppermute | solution.py:30
  61.8 8.2 %collective-permute-start.6 = (f32[3072]{0:T(1024)S(1)}, f32[3072]{0:T(1024)S(1)}, u32[]{:S(2)}, u32[]{:S(2)}) collective-permute-start(f32[3072]{0:T(1024)S(1)} %get-tuple-element.38), channel_id=1, source_target_pairs={{0,32},{32,64},{64,96},{96,128},{128,160},{160,192},{192,224},{1,3... | collective-permute-start | bytes 36872 | tf_op jit(solution)/shard_map/ppermute | solution.py:28
  67.3 6.8 %collective-permute-start.7 = (f32[3072]{0:T(1024)S(1)}, f32[3072]{0:T(1024)S(1)}, u32[]{:S(2)}, u32[]{:S(2)}) collective-permute-start(f32[3072]{0:T(1024)S(1)} %get-tuple-element.39), channel_id=1, source_target_pairs={{32,0},{64,32},{96,64},{128,96},{160,128},{192,160},{224,192},{33,... | collective-permute-start | bytes 36872 | tf_op jit(solution)/shard_map/ppermute | solution.py:30
  75.0 6.1 %collective-permute-start.9 = (f32[8448]{0:T(1024)S(1)}, f32[8448]{0:T(1024)S(1)}, u32[]{:S(2)}, u32[]{:S(2)}) collective-permute-start(f32[8448]{0:T(1024)S(1)} %reshape.527), channel_id=1, source_target_pairs={{8,0},{16,8},{24,16},{9,1},{17,9},{25,17},{10,2},{18,10},{26,18},{... | collective-permute-start | bytes 101384 | tf_op jit(solution)/shard_map/ppermute | solution.py:30
  76.9 5.3 %collective-permute-start.8 = (f32[8448]{0:T(1024)S(1)}, f32[8448]{0:T(1024)S(1)}, u32[]{:S(2)}, u32[]{:S(2)}) collective-permute-start(f32[8448]{0:T(1024)S(1)} %reshape.525), channel_id=1, source_target_pairs={{0,8},{8,16},{16,24},{1,9},{9,17},{17,25},{2,10},{10,18},{18,26},{... | collective-permute-start | bytes 101384 | tf_op jit(solution)/shard_map/ppermute | solution.py:28
  83.6 13.2 %collective-permute-start.11 = (f32[924]{0:T(1024)S(1)}, f32[924]{0:T(1024)S(1)}, u32[]{:S(2)}, u32[]{:S(2)}) collective-permute-start(f32[924]{0:T(1024)S(1)} %reshape.531), channel_id=1, source_target_pairs={{1,0},{2,1},{3,2},{4,3},{5,4},{6,5},{7,6},{9,8},{10,9},{11,10},{12... | collective-permute-start | bytes 11096 | tf_op jit(solution)/shard_map/ppermute | solution.py:30
  88.7 7.9 %collective-permute-start.10 = (f32[924]{0:T(1024)S(1)}, f32[924]{0:T(1024)S(1)}, u32[]{:S(2)}, u32[]{:S(2)}) collective-permute-start(f32[924]{0:T(1024)S(1)} %reshape.529), channel_id=1, source_target_pairs={{0,1},{1,2},{2,3},{3,4},{4,5},{5,6},{6,7},{8,9},{9,10},{10,11},{11... | collective-permute-start | bytes 11096 | tf_op jit(solution)/shard_map/ppermute | solution.py:28
  112.4 7.1 %collective-permute-start.13 = (f32[9216]{0:T(1024)S(1)}, f32[9216]{0:T(1024)S(1)}, u32[]{:S(2)}, u32[]{:S(2)}) collective-permute-start(f32[9216]{0:T(1024)S(1)} %bitcast.53), channel_id=1, source_target_pairs={{32,0},{64,32},{96,64},{128,96},{160,128},{192,160},{224,192},{33,... | collective-permute-start | bytes 110600 | tf_op jit(solution)/shard_map/ppermute | solution.py:30
  114.3 6.8 %collective-permute-start.12 = (f32[9216]{0:T(1024)S(1)}, f32[9216]{0:T(1024)S(1)}, u32[]{:S(2)}, u32[]{:S(2)}) collective-permute-start(f32[9216]{0:T(1024)S(1)} %bitcast.52), channel_id=1, source_target_pairs={{0,32},{32,64},{64,96},{96,128},{128,160},{160,192},{192,224},{1,3... | collective-permute-start | bytes 110600 | tf_op jit(solution)/shard_map/ppermute | solution.py:28
  122.1 4.4 %collective-permute-start.15 = (f32[25344]{0:T(1024)S(1)}, f32[25344]{0:T(1024)S(1)}, u32[]{:S(2)}, u32[]{:S(2)}) collective-permute-start(f32[25344]{0:T(1024)S(1)} %reshape.539), channel_id=1, source_target_pairs={{8,0},{16,8},{24,16},{9,1},{17,9},{25,17},{10,2},{18,10},{26,18},{... | collective-permute-start | bytes 304136 | tf_op jit(solution)/shard_map/ppermute | solution.py:30
  124.1 6.0 %collective-permute-start.14 = (f32[25344]{0:T(1024)S(1)}, f32[25344]{0:T(1024)S(1)}, u32[]{:S(2)}, u32[]{:S(2)}) collective-permute-start(f32[25344]{0:T(1024)S(1)} %reshape.537), channel_id=1, source_target_pairs={{0,8},{8,16},{16,24},{1,9},{9,17},{17,25},{2,10},{10,18},{18,26},{... | collective-permute-start | bytes 304136 | tf_op jit(solution)/shard_map/ppermute | solution.py:28
  130.7 8.5 %collective-permute-start.16 = (f32[2772]{0:T(1024)S(1)}, f32[2772]{0:T(1024)S(1)}, u32[]{:S(2)}, u32[]{:S(2)}) collective-permute-start(f32[2772]{0:T(1024)S(1)} %reshape.541), channel_id=1, source_target_pairs={{0,1},{1,2},{2,3},{3,4},{4,5},{5,6},{6,7},{8,9},{9,10},{10,11},{11... | collective-permute-start | bytes 33272 | tf_op jit(solution)/shard_map/ppermute | solution.py:28
  133.1 7.8 %collective-permute-start.17 = (f32[2772]{0:T(1024)S(1)}, f32[2772]{0:T(1024)S(1)}, u32[]{:S(2)}, u32[]{:S(2)}) collective-permute-start(f32[2772]{0:T(1024)S(1)} %reshape.543), channel_id=1, source_target_pairs={{1,0},{2,1},{3,2},{4,3},{5,4},{6,5},{7,6},{9,8},{10,9},{11,10},{12... | collective-permute-start | bytes 33272 | tf_op jit(solution)/shard_map/ppermute | solution.py:30
  160.4 7.4 %collective-permute-start.18 = (f32[3072]{0:T(1024)S(1)}, f32[3072]{0:T(1024)S(1)}, u32[]{:S(2)}, u32[]{:S(2)}) collective-permute-start(f32[3072]{0:T(1024)S(1)} %get-tuple-element.36), channel_id=1, source_target_pairs={{0,32},{32,64},{64,96},{96,128},{128,160},{160,192},{192,224},{1,3... | collective-permute-start | bytes 36872 | tf_op jit(solution)/shard_map/ppermute | solution.py:28
  165.8 6.8 %collective-permute-start.19 = (f32[3072]{0:T(1024)S(1)}, f32[3072]{0:T(1024)S(1)}, u32[]{:S(2)}, u32[]{:S(2)}) collective-permute-start(f32[3072]{0:T(1024)S(1)} %get-tuple-element.37), channel_id=1, source_target_pairs={{32,0},{64,32},{96,64},{128,96},{160,128},{192,160},{224,192},{33,... | collective-permute-start | bytes 36872 | tf_op jit(solution)/shard_map/ppermute | solution.py:30
  173.5 4.4 %collective-permute-start.21 = (f32[8448]{0:T(1024)S(1)}, f32[8448]{0:T(1024)S(1)}, u32[]{:S(2)}, u32[]{:S(2)}) collective-permute-start(f32[8448]{0:T(1024)S(1)} %reshape.551), channel_id=1, source_target_pairs={{8,0},{16,8},{24,16},{9,1},{17,9},{25,17},{10,2},{18,10},{26,18},{... | collective-permute-start | bytes 101384 | tf_op jit(solution)/shard_map/ppermute | solution.py:30
  175.5 5.3 %collective-permute-start.20 = (f32[8448]{0:T(1024)S(1)}, f32[8448]{0:T(1024)S(1)}, u32[]{:S(2)}, u32[]{:S(2)}) collective-permute-start(f32[8448]{0:T(1024)S(1)} %reshape.549), channel_id=1, source_target_pairs={{0,8},{8,16},{16,24},{1,9},{9,17},{17,25},{2,10},{10,18},{18,26},{... | collective-permute-start | bytes 101384 | tf_op jit(solution)/shard_map/ppermute | solution.py:28
  182.0 8.5 %collective-permute-start.22 = (f32[924]{0:T(1024)S(1)}, f32[924]{0:T(1024)S(1)}, u32[]{:S(2)}, u32[]{:S(2)}) collective-permute-start(f32[924]{0:T(1024)S(1)} %reshape.553), channel_id=1, source_target_pairs={{0,1},{1,2},{2,3},{3,4},{4,5},{5,6},{6,7},{8,9},{9,10},{10,11},{11... | collective-permute-start | bytes 11096 | tf_op jit(solution)/shard_map/ppermute | solution.py:28
  188.5 7.0 %collective-permute-start.23 = (f32[924]{0:T(1024)S(1)}, f32[924]{0:T(1024)S(1)}, u32[]{:S(2)}, u32[]{:S(2)}) collective-permute-start(f32[924]{0:T(1024)S(1)} %reshape.555), channel_id=1, source_target_pairs={{1,0},{2,1},{3,2},{4,3},{5,4},{6,5},{7,6},{9,8},{10,9},{11,10},{12... | collective-permute-start | bytes 11096 | tf_op jit(solution)/shard_map/ppermute | solution.py:30
  (11 other events, 105.4 us)
